TPU v7x, 512 devices: a whole 4x4x16 slice. The times are simulated.
512 devices in a mesh: tm: 64 (over z, y_hi, core), space: 8 (over y_lo, x).
Axes of the slice: x: 4, y: 4 (y_hi: 2, y_lo: 2; y = y_hi * 2 + y_lo), z: 16, core: 2. Of those that a mesh axis runs over, the one named last changes fastest.
Arguments:
- start_states: float32 [64, 256, 256], P('tm', 'space'), may hold values from -6 to 6
- region_map: int32 [256, 256], P('space'), may hold values from 0 to 3
- source: float32 [2, 256, 256], P(None, 'space'), may hold values from -6 to 6
- front: int32 [], replicated, may hold values from 33 to 63
Outputs:
- new_states: float32 [64, 256, 256], P('tm', 'space')
- jumps: float32 [64, 256, 256], P('tm', 'space')
All inputs are finite; a program needn't handle non-finite values.
Results may differ from a plain program's by a relative error of at most 0.000027.
Values sent between devices are 32-bit elements; how exact they have to be, the bound alone decides.
No kernel may reach another device: no remote copies, remote signals or barrier semaphores. Data moves between devices by JAX's collectives and lax.ppermute only.
A program may use at most 64 MiB of HBM per device.

v0:
```python
import math

import jax
import jax.numpy as jnp
from jax import lax
from jax.sharding import PartitionSpec as P

FINE = 16
ITERS = 2


RELUCTIVITY = (1.0, 0.3, 1.0, 0.25)
SATURATION = (0.0, 2.0, 0.0, 1.5)
MOBILITY = (0.15, 0.02, 0.0004, 0.0008)


def extended_2(block, sides, width):
    for axis, dim in sides:
        count = lax.axis_size(axis)
        forward = [(i, i + 1) for i in range(count - 1)]
        backward = [(target, source) for source, target in forward]
        low = lax.ppermute(
            lax.slice_in_dim(block, block.shape[dim] - width, None, axis=dim), axis, forward
        )
        high = lax.ppermute(lax.slice_in_dim(block, 0, width, axis=dim), axis, backward)
        block = jnp.concatenate([low, block, high], axis=dim)
    return block


def entering(x, axis, combine, identity):
    size, position = (lax.axis_size(axis), lax.axis_index(axis))
    everything = jax.tree.map(lambda part: lax.all_gather(part, axis), x)
    start = jax.tree.map(
        lambda part, zero: jnp.broadcast_to(jnp.asarray(zero, part.dtype), part.shape), x, identity
    )

    def hop(k, before):
        reached = k < position
        new = combine(before, jax.tree.map(lambda part: part[k], everything))
        return jax.tree.map(lambda a, b: jnp.where(reached, a, b), new, before)

    return lax.fori_loop(0, size, hop, start)


def from_root(x, axis, root):
    mine = lax.axis_index(axis) == root
    return lax.psum(jnp.where(mine, x, jnp.zeros_like(x)), axis)


def from_behind(x, axis, by):
    size = lax.axis_size(axis)
    return lax.ppermute(x, axis, [(i, (i + by) % size) for i in range(size)])


def lookup(region_map, table):
    result = jnp.zeros(region_map.shape, jnp.float32)
    for region, entry_value in enumerate(table):
        result = result + jnp.where(
            region_map == region, jnp.float32(entry_value), jnp.float32(0.0)
        )
    return result


def flux_terms(extended, reluctivity, saturation):
    field_cols = jnp.pad(extended, ((0, 0), (1, 1)))
    relu_cols = jnp.pad(reluctivity, ((0, 0), (1, 1)))
    satu_cols = jnp.pad(saturation, ((0, 0), (1, 1)))
    center = field_cols[1:-1, 1:-1]
    own_rel = relu_cols[1:-1, 1:-1]
    own_sat = satu_cols[1:-1, 1:-1]
    divergence = jnp.zeros_like(center)
    diagonal = jnp.zeros_like(center)
    for row_part, col_part in (
        (slice(0, -2), slice(1, -1)),
        (slice(2, None), slice(1, -1)),
        (slice(1, -1), slice(0, -2)),
        (slice(1, -1), slice(2, None)),
    ):
        difference = field_cols[row_part, col_part] - center
        square = difference * difference
        face_rel = 0.5 * (own_rel + relu_cols[row_part, col_part])
        face_sat = 0.5 * (own_sat + satu_cols[row_part, col_part])
        weight = face_rel * (1.0 + face_sat * square / (1.0 + square))
        divergence = divergence + weight * difference
        diagonal = diagonal + weight
    return (divergence, diagonal)


def compose_maps(earlier, later):
    return (later[0] * earlier[0], later[0] * earlier[1] + later[1])


def on_device(start_states, region_map, source, front):
    field_now = start_states[0]
    slices = lax.axis_size("tm")
    slice_index = lax.axis_index("tm")
    scale = 2.0 * math.pi / (slices * FINE)
    stacked = jnp.stack(
        [
            lookup(region_map, RELUCTIVITY),
            lookup(region_map, SATURATION),
            lookup(region_map, MOBILITY),
            source[0],
            source[1],
        ],
        0,
    )
    padded_fields = extended_2(stacked, (("space", 1),), 1)
    mobile = stacked[2]

    def advance(block, values, divergence, step_index):
        phase_angle = (slice_index * FINE + step_index).astype(jnp.float32) * scale
        current = block[3] * jnp.cos(phase_angle) + block[4] * jnp.sin(phase_angle)
        return values + block[2] * (divergence + current)

    def single_step(values, step_index):
        extended = extended_2(values, (("space", 0),), 1)
        divergence, diagonal = flux_terms(extended, padded_fields[0], padded_fields[1])
        return (advance(stacked, values, divergence, step_index), diagonal)

    cut_slice = (front - 1) % slices
    keep_map = slice_index != cut_slice
    fine_end = field_now
    for sweep in range(ITERS):
        fine_values = field_now
        fine_values, fine_diagonal = single_step(fine_values, 0)

        def single_turn(counter, current_values):
            return single_step(current_values, counter)[0]

        fine_values = lax.fori_loop(1, FINE, single_turn, fine_values)
        fine_end = fine_values
        diagonal = fine_diagonal
        decay = 1.0 / (1.0 + FINE * mobile * diagonal)
        decay = jnp.where(keep_map, decay, 0.0)
        offset = fine_end - decay * field_now
        prefix = entering(
            (decay, offset), "tm", compose_maps, (jnp.ones_like(decay), jnp.zeros_like(offset))
        )
        total = compose_maps(prefix, (decay, offset))
        closing = from_root(total[1], "tm", slices - 1)
        field_now = prefix[0] * closing + prefix[1]
    jumps = from_behind(fine_end, "tm", 1) - field_now
    return (field_now[None], jumps[None])


def solution(mesh):
    placed = (P("tm", "space", None), P("space", None), P(None, "space", None), P())
    return jax.shard_map(
        on_device,
        mesh=mesh,
        in_specs=placed,
        out_specs=(P("tm", "space", None), P("tm", "space", None)),
        check_vma=False,
    )
```

profile of v0, /device:TPU:7, one launch (start us, length us, event | category | flops | bytes accessed | tf_op | source)
XLA Modules:
  0.0 1530.4 jit_solution(15619786963016849872)
XLA Ops:
  8.8 3.1 collective-permute-start.4
  11.9 2.2 collective-permute-start.6
  14.8 5.2 collective-permute-start.5
  23.6 2.9 collective-permute-done.7
  29.3 129.0 %while.62 = (s32[]{:T(128)}, f32[32,256]{1,0:T(8,128)S(1)}, f32[32,256]{1,0:T(8,128)S(1)}, f32[32,256]{1,0:T(8,128)S(1)}, f32[32,256]{1,0:T(8,128)S(1)}, /*index...) while((s32[]{:T(128)}, f32[32,256]{1,0:T(8,128)S(1)}, ...), condition=%wide.region_1.2_spmd, body=%wide.region_0.1_spmd.sunk | while | flops 520741 | bytes 784917 | solution.py:131
  31.3 5.5 collective-permute-start.1
  39.6 5.7 collective-permute-start.1
  48.2 5.7 collective-permute-start.1
  56.9 5.7 collective-permute-start.1
  65.5 5.7 collective-permute-start.1
  74.1 5.7 collective-permute-start.1
  82.7 5.7 collective-permute-start.1
  91.3 5.7 collective-permute-start.1
  99.9 5.7 collective-permute-start.1
  108.6 5.7 collective-permute-start.1
  117.2 5.7 collective-permute-start.1
  125.8 5.7 collective-permute-start.1
  134.4 5.7 collective-permute-start.1
  143.0 5.7 collective-permute-start.1
  151.6 5.7 collective-permute-start.1
  159.9 167.5 %all-gather.9.cloned.1.call-done = f32[2048,256]{1,0:T(8,128)} async-done(((f32[32,256]{1,0:T(8,128)}), f32[2048,256]{1,0:T(8,128)}) %all-gather.9.cloned.1.call-update) | async-done | bytes 2097168 | tf_op jit(solution)/shard_map/all_gather | solution.py:32
  327.3 142.1 %all-gather.11.cloned.1.call-done = f32[2048,256]{1,0:T(8,128)} async-done(((f32[32,256]{1,0:T(8,128)}), f32[2048,256]{1,0:T(8,128)}) %all-gather.11.cloned.1.call-update) | async-done | bytes 2097168 | tf_op jit(solution)/shard_map/all_gather | solution.py:32
  469.4 52.4 %while.64 = (s32[]{:T(128)}, f32[32,256]{1,0:T(8,128)S(1)}, f32[32,256]{1,0:T(8,128)S(1)}, s32[]{:T(128)}, f32[64,32,256]{2,1,0:T(8,128)}, /*index=5*/f32[64,32,256]{2,1,0:T(8,128)}, s32[]{:T(128)}, s32[]{:T(128)}) while((s32[]{:T(128)}, f32[32,256]{1,0:T(8,128)S(1)}, f32[32,256]{1,0:T(8,128)S(1)}, s32[]{:T(128)}, ...), condition=%wide.region_3.4_spmd.clone, body=%wide.region_2.3_spmd.clone.sunk | while | flops 57348 | bytes 196717 | solution.py:42
  522.5 251.5 %psum.14 = f32[32,256]{1,0:T(8,128)S(1)} all-reduce(f32[32,256]{1,0:T(8,128)S(1)} %add_select_fusion.1), channel_id=1, replica_groups=mesh['tm'=64,'space'=8] {'tm'}, use_global_device_ids=true, to_apply=%region_4.5 | all-reduce | flops 8192 | bytes 65536 | tf_op jit(solution)/shard_map/psum | solution.py:47
  774.0 3.1 collective-permute-start.8
  777.1 2.2 collective-permute-start.9
  779.3 4.2 collective-permute-done.9
  783.8 129.0 %while.63 = (s32[]{:T(128)}, f32[32,256]{1,0:T(8,128)S(1)}, f32[32,256]{1,0:T(8,128)S(1)}, f32[32,256]{1,0:T(8,128)S(1)}, f32[32,256]{1,0:T(8,128)S(1)}, /*index...) while((s32[]{:T(128)}, f32[32,256]{1,0:T(8,128)S(1)}, ...), condition=%wide.region_6.7_spmd, body=%wide.region_5.6_spmd.sunk | while | flops 520741 | bytes 784917 | solution.py:131
  785.8 5.5 collective-permute-start.3
  794.1 5.7 collective-permute-start.3
  802.8 5.7 collective-permute-start.3
  811.4 5.7 collective-permute-start.3
  820.0 5.7 collective-permute-start.3
  828.6 5.7 collective-permute-start.3
  837.2 5.7 collective-permute-start.3
  845.8 5.7 collective-permute-start.3
  854.4 5.7 collective-permute-start.3
  863.1 5.7 collective-permute-start.3
  871.7 5.7 collective-permute-start.3
  880.3 5.7 collective-permute-start.3
  888.9 5.7 collective-permute-start.3
  897.5 5.7 collective-permute-start.3
  906.1 5.7 collective-permute-start.3
  914.1 24.4 %collective-permute-start.10 = (f32[32,256]{1,0:T(8,128)S(1)}, f32[32,256]{1,0:T(8,128)S(1)}, u32[]{:S(2)}, u32[]{:S(2)}) collective-permute-start(f32[32,256]{1,0:T(8,128)S(1)} %get-tuple-element.623), channel_id=1, source_target_pairs={{0,8},{8,16},{16,24},{24,32},{32,40},{40,48},{48,56},{56,64},{64,7... | collective-permute-start | bytes 98312 | tf_op jit(solution)/shard_map/ppermute | solution.py:52
  938.5 138.2 %all-gather.13.cloned.1.call-done = f32[2048,256]{1,0:T(8,128)} async-done(((f32[32,256]{1,0:T(8,128)}), f32[2048,256]{1,0:T(8,128)}) %all-gather.13.cloned.1.call-update) | async-done | bytes 2097168 | tf_op jit(solution)/shard_map/all_gather | solution.py:32
  1076.7 141.9 %all-gather.15.cloned.1.call-done = f32[2048,256]{1,0:T(8,128)} async-done(((f32[32,256]{1,0:T(8,128)}), f32[2048,256]{1,0:T(8,128)}) %all-gather.15.cloned.1.call-update) | async-done | bytes 2097168 | tf_op jit(solution)/shard_map/all_gather | solution.py:32
  1218.6 52.4 %while.65 = (s32[]{:T(128)}, f32[32,256]{1,0:T(8,128)S(1)}, f32[32,256]{1,0:T(8,128)S(1)}, s32[]{:T(128)}, f32[64,32,256]{2,1,0:T(8,128)}, /*index=5*/f32[64,32,256]{2,1,0:T(8,128)}, s32[]{:T(128)}, s32[]{:T(128)}) while((s32[]{:T(128)}, f32[32,256]{1,0:T(8,128)S(1)}, f32[32,256]{1,0:T(8,128)S(1)}, s32[]{:T(128)}, ...), condition=%wide.region_8.9_spmd.clone, body=%wide.region_7.8_spmd.clone.sunk | while | flops 57348 | bytes 196717 | solution.py:42
  1271.8 251.5 %psum.15 = f32[32,256]{1,0:T(8,128)S(1)} all-reduce(f32[32,256]{1,0:T(8,128)S(1)} %add_select_fusion), channel_id=1, replica_groups=mesh['tm'=64,'space'=8] {'tm'}, use_global_device_ids=true, to_apply=%region_9.10 | all-reduce | flops 8192 | bytes 65536 | tf_op jit(solution)/shard_map/psum | solution.py:47
  (408 shorter events, 194.9 us)
Async XLA Ops:
  7.2 320.1 %all-gather.9.cloned.1.call-start = ((), (), s32[]{:S(2)}) async-start(), calls=%async_computation | async-start | bytes 2129920 | tf_op jit(solution)/shard_map/all_gather | solution.py:32
  8.8 18.5 %collective-permute-start.4 = (f32[5,1,256]{2,1,0:T(1,128)S(1)}, f32[5,1,256]{2,1,0:T(1,128)S(1)}, u32[]{:S(2)}, u32[]{:S(2)}) collective-permute-start(f32[5,1,256]{2,1,0:T(1,128)S(1)} %get-tuple-element.769), channel_id=1, source_target_pairs={{0,1},{1,2},{2,3},{3,4},{4,5},{5,6},{6,7},{8,9},{9,10},{10,11},{11... | collective-permute-start | bytes 15368 | tf_op jit(solution)/shard_map/ppermute | solution.py:22
  11.9 15.4 %collective-permute-start.6 = (f32[5,1,256]{2,1,0:T(1,128)S(1)}, f32[5,1,256]{2,1,0:T(1,128)S(1)}, u32[]{:S(2)}, u32[]{:S(2)}) collective-permute-start(f32[5,1,256]{2,1,0:T(1,128)S(1)} %get-tuple-element.770), channel_id=1, source_target_pairs={{1,0},{2,1},{3,2},{4,3},{5,4},{6,5},{7,6},{9,8},{10,9},{11,10},{12... | collective-permute-start | bytes 15368 | tf_op jit(solution)/shard_map/ppermute | solution.py:25
  14.8 8.8 collective-permute-start.5
  29.3 7.6 collective-permute-start
  37.7 7.8 collective-permute-start
  39.6 6.4 collective-permute-start.1
  46.3 7.8 collective-permute-start
  48.2 6.4 collective-permute-start.1
  54.9 7.8 collective-permute-start
  63.5 7.8 collective-permute-start
  65.5 6.4 collective-permute-start.1
  72.2 7.8 collective-permute-start
  74.1 6.4 collective-permute-start.1
  80.8 7.8 collective-permute-start
  82.7 6.4 collective-permute-start.1
  89.4 7.8 collective-permute-start
  91.3 6.4 collective-permute-start.1
  98.0 7.8 collective-permute-start
  99.9 6.4 collective-permute-start.1
  106.6 7.8 collective-permute-start
  108.6 6.4 collective-permute-start.1
  115.2 7.8 collective-permute-start
  123.9 7.8 collective-permute-start
  125.8 6.4 collective-permute-start.1
  132.5 7.8 collective-permute-start
  134.4 6.4 collective-permute-start.1
  141.1 7.8 collective-permute-start
  149.7 7.8 collective-permute-start
  159.0 310.3 %all-gather.11.cloned.1.call-start = ((), (), s32[]{:S(2)}) async-start(), calls=%async_computation.1 | async-start | bytes 2129920 | tf_op jit(solution)/shard_map/all_gather | solution.py:32
  159.8 916.9 %all-gather.13.cloned.1.call-start = ((), (), s32[]{:S(2)}) async-start(), calls=%async_computation.2 | async-start | bytes 2129920 | tf_op jit(solution)/shard_map/all_gather | solution.py:32
  783.8 7.6 collective-permute-start.2
  792.2 7.8 collective-permute-start.2
  800.8 7.8 collective-permute-start.2
  809.4 7.8 collective-permute-start.2
  818.1 7.8 collective-permute-start.2
  826.7 7.8 collective-permute-start.2
  835.3 7.8 collective-permute-start.2
  843.9 7.8 collective-permute-start.2
  852.5 7.8 collective-permute-start.2
  861.1 7.8 collective-permute-start.2
  869.7 7.8 collective-permute-start.2
  878.4 7.8 collective-permute-start.2
  887.0 7.8 collective-permute-start.2
  895.6 7.8 collective-permute-start.2
  904.2 7.8 collective-permute-start.2
  913.5 305.1 %all-gather.15.cloned.1.call-start = ((), (), s32[]{:S(2)}) async-start(), calls=%async_computation.3 | async-start | bytes 2129920 | tf_op jit(solution)/shard_map/all_gather | solution.py:32
  914.1 609.1 %collective-permute-start.10 = (f32[32,256]{1,0:T(8,128)S(1)}, f32[32,256]{1,0:T(8,128)S(1)}, u32[]{:S(2)}, u32[]{:S(2)}) collective-permute-start(f32[32,256]{1,0:T(8,128)S(1)} %get-tuple-element.623), channel_id=1, source_target_pairs={{0,8},{8,16},{16,24},{24,32},{32,40},{40,48},{48,56},{56,64},{64,7... | collective-permute-start | bytes 98312 | tf_op jit(solution)/shard_map/ppermute | solution.py:52
  (25 other events, 900.5 us)
Sparse Core Ops, SparseCore 0:
  159.2 168.1 all-gather.8
  331.2 138.1 all-gather.10
  913.6 162.9 all-gather.12
  1080.4 138.1 all-gather.14
where the time goes:
time: 1550 us; the launch traced here: 1530 us
  waiting for transfers between devices  614 us (40%)
  blocking collectives  503 us (32%)
  starting transfers between devices  271 us (17%)
  other arithmetic  116 us (7%)
    all_gather x4, waiting for transfers between devices, entering(): everything = jax.tree.map(lambda part: lax.all_gather(part, axis), x)  590 us
    psum x2, blocking collectives, from_root(): return lax.psum(jnp.where(mine, x, jnp.zeros_like(x)), axis)  503 us
    ppermute x33, starting transfers between devices, extended_2(): lax.ppermute(lax.slice_in_dim(block, block.shape[dim] - width, None, axis...  182 us
    select_n x128, other arithmetic, hop(): return jax.tree.map(lambda a, b: jnp.where(reached, a, b), new, before)  102 us
    ppermute x33, starting transfers between devices, extended_2(): lax.ppermute(lax.slice_in_dim(block, 0, width, axis=dim), axis, backward)  63.9 us
  transfers between devices with their start and end apart: 71, of which 36 were waited for; matrix products, arithmetic and copies ran while one was open for 4% of the time, Pallas kernels for 0%

commit v1 on v0

v1 whole, which is shorter than its diff:
```python
import math

import jax
import jax.numpy as jnp
from jax import lax
from jax.sharding import PartitionSpec as P

FINE = 16
ITERS = 2
SCAN_RADIX = 4


RELUCTIVITY = (1.0, 0.3, 1.0, 0.25)
SATURATION = (0.0, 2.0, 0.0, 1.5)
MOBILITY = (0.15, 0.02, 0.0004, 0.0008)


def with_halo(block, width):
    count = lax.axis_size("space")
    rows = block.shape[-2]
    forward = [(i, i + 1) for i in range(count - 1)]
    backward = [(i + 1, i) for i in range(count - 1)]
    above = lax.ppermute(lax.slice_in_dim(block, rows - width, rows, axis=block.ndim - 2), "space", forward)
    below = lax.ppermute(lax.slice_in_dim(block, 0, width, axis=block.ndim - 2), "space", backward)
    return jnp.concatenate([above, block, below], axis=block.ndim - 2)


def lookup_shifted(code, table):
    result = jnp.zeros(code.shape, jnp.float32)
    for region, entry_value in enumerate(table):
        result = result + jnp.where(code == jnp.float32(region + 1), jnp.float32(entry_value), jnp.float32(0.0))
    return result


def face_terms(values, axis):
    pad = [(0, 0)] * values.ndim
    pad[axis] = (1, 1)
    padded = jnp.pad(values, pad)
    n = padded.shape[axis]
    return 0.5 * (lax.slice_in_dim(padded, 0, n - 1, axis=axis) + lax.slice_in_dim(padded, 1, n, axis=axis))


def flux_terms(field, row_rel, row_sat, col_rel, col_sat):
    rows, cols = field.shape
    rpad = jnp.pad(field, ((1, 1), (0, 0)))
    row_diff = rpad[1:] - rpad[:-1]
    row_sq = row_diff * row_diff
    row_w = row_rel * (1.0 + row_sat * row_sq / (1.0 + row_sq))
    row_flux = row_w * row_diff
    cpad = jnp.pad(field, ((0, 0), (1, 1)))
    col_diff = cpad[:, 1:] - cpad[:, :-1]
    col_sq = col_diff * col_diff
    col_w = col_rel * (1.0 + col_sat * col_sq / (1.0 + col_sq))
    col_flux = col_w * col_diff
    divergence = (((-row_flux[:-1]) + row_flux[1:]) + (-col_flux[:, :-1])) + col_flux[:, 1:]
    diagonal = ((row_w[:-1] + row_w[1:]) + col_w[:, :-1]) + col_w[:, 1:]
    return divergence, diagonal


def compose_maps(earlier, later):
    return (later[0] * earlier[0], later[0] * earlier[1] + later[1])


def periodic_states(decay, offset, extra):
    count = lax.axis_size("tm")

    def from_behind(x, by):
        return lax.ppermute(x, "tm", [(i, (i + by) % count) for i in range(count)])

    own = jnp.stack([decay, offset])
    first = min(SCAN_RADIX, count)
    got = [from_behind(jnp.stack([decay, offset] + extra), 1)]
    got += [from_behind(own, by) for by in range(2, first + 1)]
    carried = [part[2:] for part in got[:1]]
    window = (got[-1][0], got[-1][1])
    for part in reversed(got[:-1]):
        window = compose_maps(window, (part[0], part[1]))
    length = first
    while length < count:
        parts = [from_behind(jnp.stack(window), by * length) for by in range(1, SCAN_RADIX) if by * length < count]
        joined = (parts[-1][0], parts[-1][1])
        for part in reversed(parts[:-1]):
            joined = compose_maps(joined, (part[0], part[1]))
        window = compose_maps(joined, window)
        length = length * (len(parts) + 1)
    return window[1], (carried[0] if extra else None)


def on_device(start_states, region_map, source, front):
    field_now = start_states[0]
    rows, cols = field_now.shape
    width = FINE
    slices = lax.axis_size("tm")
    slice_index = lax.axis_index("tm")
    scale = 2.0 * math.pi / (slices * FINE)

    stacked = jnp.stack(
        [field_now, region_map.astype(jnp.float32) + 1.0, source[0], source[1]], 0
    )
    extended = with_halo(stacked, width)
    code = extended[1]
    reluct = lookup_shifted(code, RELUCTIVITY)
    satur = lookup_shifted(code, SATURATION)
    mobile_ext = lookup_shifted(code, MOBILITY)
    src_cos, src_sin = extended[2], extended[3]
    row_rel = face_terms(reluct, 0)
    row_sat = face_terms(satur, 0)
    col_rel = face_terms(reluct, 1)
    col_sat = face_terms(satur, 1)
    mobile = mobile_ext[width : width + rows]

    def single_step(values, step_index):
        divergence, diagonal = flux_terms(values, row_rel, row_sat, col_rel, col_sat)
        phase_angle = (slice_index * FINE + step_index).astype(jnp.float32) * scale
        current = src_cos * jnp.cos(phase_angle) + src_sin * jnp.sin(phase_angle)
        return values + mobile_ext * (divergence + current), diagonal

    cut_slice = (front - 1) % slices
    keep_map = slice_index != cut_slice
    values_ext = extended[0]
    for sweep in range(ITERS):
        if sweep > 0:
            values_ext = with_halo(field_now, width)
        fine_values, fine_diagonal = single_step(values_ext, 0)
        for step_index in range(1, FINE):
            fine_values = single_step(fine_values, step_index)[0]
        fine_end = fine_values[width : width + rows]
        diagonal = fine_diagonal[width : width + rows]
        decay = 1.0 / (1.0 + FINE * mobile * diagonal)
        decay = jnp.where(keep_map, decay, 0.0)
        offset = fine_end - decay * field_now
        last = sweep == ITERS - 1
        field_now, previous_end = periodic_states(decay, offset, [fine_end] if last else [])
    jumps = previous_end[0] - field_now
    return (field_now[None], jumps[None])


def solution(mesh):
    placed = (P("tm", "space", None), P("space", None), P(None, "space", None), P())
    return jax.shard_map(
        on_device,
        mesh=mesh,
        in_specs=placed,
        out_specs=(P("tm", "space", None), P("tm", "space", None)),
        check_vma=False,
    )
```

time: 1550 us -> 161 us (0.10)
  the two profiles are of different devices: /device:TPU:7 before, /device:TPU:8 now
where the time goes in v1:
time: 161 us; the launch traced here: 160 us
  starting transfers between devices  105 us (65%)
  waiting for transfers between devices  39.6 us (25%)
  other arithmetic  10.3 us (6%)
  between operations  4.69 us (3%)
    ppermute x20, starting transfers between devices, from_behind(): return lax.ppermute(x, 'tm', [(i, (i + by) % count) for i in range(count)])  92.8 us
    ppermute x20, waiting for transfers between devices, from_behind(): return lax.ppermute(x, 'tm', [(i, (i + by) % count) for i in range(count)])  31.4 us
    ppermute x2, waiting for transfers between devices, with_halo(): lax.ppermute(lax.slice_in_dim(block, rows - width, rows, axis=block.ndim...  8.23 us
    ppermute x2, starting transfers between devices, with_halo(): lax.ppermute(lax.slice_in_dim(block, 0, width, axis=block.ndim - 2), 'spa...  7.73 us
    ppermute x2, starting transfers between devices, with_halo(): lax.ppermute(lax.slice_in_dim(block, rows - width, rows, axis=block.ndim...  4.58 us
    mul x32, other arithmetic, flux_terms(): col_flux = col_w * col_diff  3.56 us
  transfers between devices with their start and end apart: 24, of which 12 were waited for; matrix products, arithmetic and copies ran while one was open for 0% of the time, Pallas kernels for 0%

profile of v1, /device:TPU:8, one launch (start us, length us, event | category | flops | bytes accessed | tf_op | source)
XLA Modules:
  0.0 160.0 jit_solution(12903615906200050708)
XLA Ops:
  0.6 0.8 add_bitcast_fusion.3
  1.4 0.8 pad_maximum_fusion.1
  2.3 4.6 %collective-permute-start.1 = (f32[4,16,256]{2,1,0:T(8,128)S(1)}, f32[4,16,256]{2,1,0:T(8,128)S(1)}, u32[]{:S(2)}, u32[]{:S(2)}) collective-permute-start(f32[4,16,256]{2,1,0:T(8,128)S(1)} %get-tuple-element.42), channel_id=1, source_target_pairs={{1,0},{2,1},{3,2},{4,3},{5,4},{6,5},{7,6},{9,8},{10,9},{11,10},{12... | collective-permute-start | bytes 196616 | tf_op jit(solution)/shard_map/ppermute | solution.py:24
  6.8 1.9 %collective-permute-start = (f32[4,16,256]{2,1,0:T(8,128)S(1)}, f32[4,16,256]{2,1,0:T(8,128)S(1)}, u32[]{:S(2)}, u32[]{:S(2)}) collective-permute-start(f32[4,16,256]{2,1,0:T(8,128)S(1)} %get-tuple-element.41), channel_id=1, source_target_pairs={{0,1},{1,2},{2,3},{3,4},{4,5},{5,6},{6,7},{8,9},{9,10},{10,11},{11... | collective-permute-start | bytes 196616 | tf_op jit(solution)/shard_map/ppermute | solution.py:23
  11.9 3.2 %collective-permute-done = f32[4,16,256]{2,1,0:T(8,128)S(1)} collective-permute-done((f32[4,16,256]{2,1,0:T(8,128)S(1)}, f32[4,16,256]{2,1,0:T(8,128)S(1)}, u32[]{:S(2)}, u32[]{:S(2)}) %collective-permute-start) | collective-permute-done | bytes 65568 | tf_op jit(solution)/shard_map/ppermute | solution.py:23
  15.3 0.2 fusion.198
  16.4 0.1 multiply_multiply_fusion.26
  16.9 0.1 multiply_multiply_fusion.24
  17.7 0.1 multiply_multiply_fusion.21
  18.2 0.1 multiply_multiply_fusion.19
  18.7 0.1 multiply_multiply_fusion.17
  19.6 3.8 %collective-permute-start.5 = (f32[2,32,256]{2,1,0:T(8,128)S(1)}, f32[2,32,256]{2,1,0:T(8,128)S(1)}, u32[]{:S(2)}, u32[]{:S(2)}) collective-permute-start(f32[2,32,256]{2,1,0:T(8,128)S(1)} %pad_maximum_fusion.3), channel_id=1, source_target_pairs={{0,32},{8,40},{16,48},{24,56},{32,64},{40,72},{48,80},{56,88},{64,... | collective-permute-start | bytes 196616 | tf_op jit(solution)/shard_map/ppermute | solution.py:68
  23.4 2.2 %collective-permute-start.4 = (f32[2,32,256]{2,1,0:T(8,128)S(1)}, f32[2,32,256]{2,1,0:T(8,128)S(1)}, u32[]{:S(2)}, u32[]{:S(2)}) collective-permute-start(f32[2,32,256]{2,1,0:T(8,128)S(1)} %pad_maximum_fusion.3), channel_id=1, source_target_pairs={{0,24},{8,32},{16,40},{24,48},{32,56},{40,64},{48,72},{56,80},{64,... | collective-permute-start | bytes 196616 | tf_op jit(solution)/shard_map/ppermute | solution.py:68
  25.6 4.2 %collective-permute-start.3 = (f32[2,32,256]{2,1,0:T(8,128)S(1)}, f32[2,32,256]{2,1,0:T(8,128)S(1)}, u32[]{:S(2)}, u32[]{:S(2)}) collective-permute-start(f32[2,32,256]{2,1,0:T(8,128)S(1)} %pad_maximum_fusion.3), channel_id=1, source_target_pairs={{0,16},{8,24},{16,32},{24,40},{32,48},{40,56},{48,64},{56,72},{64,... | collective-permute-start | bytes 196616 | tf_op jit(solution)/shard_map/ppermute | solution.py:68
  29.9 3.6 %collective-permute-start.2 = (f32[2,32,256]{2,1,0:T(8,128)S(1)}, f32[2,32,256]{2,1,0:T(8,128)S(1)}, u32[]{:S(2)}, u32[]{:S(2)}) collective-permute-start(f32[2,32,256]{2,1,0:T(8,128)S(1)} %pad_maximum_fusion.3), channel_id=1, source_target_pairs={{0,8},{8,16},{16,24},{24,32},{32,40},{40,48},{48,56},{56,64},{64,7... | collective-permute-start | bytes 196616 | tf_op jit(solution)/shard_map/ppermute | solution.py:68
  33.6 6.2 %collective-permute-done.3 = f32[2,32,256]{2,1,0:T(8,128)S(1)} collective-permute-done((f32[2,32,256]{2,1,0:T(8,128)S(1)}, f32[2,32,256]{2,1,0:T(8,128)S(1)}, u32[]{:S(2)}, u32[]{:S(2)}) %collective-permute-start.3) | collective-permute-done | bytes 65568 | tf_op jit(solution)/shard_map/ppermute | solution.py:68
  39.8 5.8 %collective-permute-start.8 = (f32[2,32,256]{2,1,0:T(8,128)S(1)}, f32[2,32,256]{2,1,0:T(8,128)S(1)}, u32[]{:S(2)}, u32[]{:S(2)}) collective-permute-start(f32[2,32,256]{2,1,0:T(8,128)S(1)} %pad_maximum_fusion.4), channel_id=1, source_target_pairs={{0,96},{8,104},{16,112},{24,120},{32,128},{40,136},{48,144},{56,15... | collective-permute-start | bytes 196616 | tf_op jit(solution)/shard_map/ppermute | solution.py:68
  45.6 5.2 %collective-permute-start.7 = (f32[2,32,256]{2,1,0:T(8,128)S(1)}, f32[2,32,256]{2,1,0:T(8,128)S(1)}, u32[]{:S(2)}, u32[]{:S(2)}) collective-permute-start(f32[2,32,256]{2,1,0:T(8,128)S(1)} %pad_maximum_fusion.4), channel_id=1, source_target_pairs={{0,64},{8,72},{16,80},{24,88},{32,96},{40,104},{48,112},{56,120},{... | collective-permute-start | bytes 196616 | tf_op jit(solution)/shard_map/ppermute | solution.py:68
  50.8 5.0 %collective-permute-start.6 = (f32[2,32,256]{2,1,0:T(8,128)S(1)}, f32[2,32,256]{2,1,0:T(8,128)S(1)}, u32[]{:S(2)}, u32[]{:S(2)}) collective-permute-start(f32[2,32,256]{2,1,0:T(8,128)S(1)} %pad_maximum_fusion.4), channel_id=1, source_target_pairs={{0,32},{8,40},{16,48},{24,56},{32,64},{40,72},{48,80},{56,88},{64,... | collective-permute-start | bytes 196616 | tf_op jit(solution)/shard_map/ppermute | solution.py:68
  55.9 2.3 %collective-permute-done.6 = f32[2,32,256]{2,1,0:T(8,128)S(1)} collective-permute-done((f32[2,32,256]{2,1,0:T(8,128)S(1)}, f32[2,32,256]{2,1,0:T(8,128)S(1)}, u32[]{:S(2)}, u32[]{:S(2)}) %collective-permute-start.6) | collective-permute-done | bytes 65568 | tf_op jit(solution)/shard_map/ppermute | solution.py:68
  58.2 7.5 %collective-permute-start.9 = (f32[2,32,256]{2,1,0:T(8,128)S(1)}, f32[2,32,256]{2,1,0:T(8,128)S(1)}, u32[]{:S(2)}, u32[]{:S(2)}) collective-permute-start(f32[2,32,256]{2,1,0:T(8,128)S(1)} %pad_maximum_fusion.5), channel_id=1, source_target_pairs={{0,128},{8,136},{16,144},{24,152},{32,160},{40,168},{48,176},{56,1... | collective-permute-start | bytes 196616 | tf_op jit(solution)/shard_map/ppermute | solution.py:68
  65.7 4.0 %collective-permute-start.10 = (f32[2,32,256]{2,1,0:T(8,128)S(1)}, f32[2,32,256]{2,1,0:T(8,128)S(1)}, u32[]{:S(2)}, u32[]{:S(2)}) collective-permute-start(f32[2,32,256]{2,1,0:T(8,128)S(1)} %pad_maximum_fusion.5), channel_id=1, source_target_pairs={{0,256},{8,264},{16,272},{24,280},{32,288},{40,296},{48,304},{56,3... | collective-permute-start | bytes 196616 | tf_op jit(solution)/shard_map/ppermute | solution.py:68
  69.7 7.6 %collective-permute-start.11 = (f32[2,32,256]{2,1,0:T(8,128)S(1)}, f32[2,32,256]{2,1,0:T(8,128)S(1)}, u32[]{:S(2)}, u32[]{:S(2)}) collective-permute-start(f32[2,32,256]{2,1,0:T(8,128)S(1)} %pad_maximum_fusion.5), channel_id=1, source_target_pairs={{0,384},{8,392},{16,400},{24,408},{32,416},{40,424},{48,432},{56,4... | collective-permute-start | bytes 196616 | tf_op jit(solution)/shard_map/ppermute | solution.py:68
  77.3 4.6 %collective-permute-done.10 = f32[2,32,256]{2,1,0:T(8,128)S(1)} collective-permute-done((f32[2,32,256]{2,1,0:T(8,128)S(1)}, f32[2,32,256]{2,1,0:T(8,128)S(1)}, u32[]{:S(2)}, u32[]{:S(2)}) %collective-permute-start.10) | collective-permute-done | bytes 65568 | tf_op jit(solution)/shard_map/ppermute | solution.py:68
  81.9 1.5 collective-permute-done.11
  83.4 3.2 %collective-permute-start.13 = (f32[16,256]{1,0:T(8,128)S(1)}, f32[16,256]{1,0:T(8,128)S(1)}, u32[]{:S(2)}, u32[]{:S(2)}) collective-permute-start(f32[16,256]{1,0:T(8,128)S(1)} %get-tuple-element.62), channel_id=1, source_target_pairs={{1,0},{2,1},{3,2},{4,3},{5,4},{6,5},{7,6},{9,8},{10,9},{11,10},{12... | collective-permute-start | bytes 49160 | tf_op jit(solution)/shard_map/ppermute | solution.py:24
  86.6 2.7 %collective-permute-start.12 = (f32[16,256]{1,0:T(8,128)S(1)}, f32[16,256]{1,0:T(8,128)S(1)}, u32[]{:S(2)}, u32[]{:S(2)}) collective-permute-start(f32[16,256]{1,0:T(8,128)S(1)} %get-tuple-element.61), channel_id=1, source_target_pairs={{0,1},{1,2},{2,3},{3,4},{4,5},{5,6},{6,7},{8,9},{9,10},{10,11},{11... | collective-permute-start | bytes 49160 | tf_op jit(solution)/shard_map/ppermute | solution.py:23
  89.3 5.1 %collective-permute-done.12 = f32[16,256]{1,0:T(8,128)S(1)} collective-permute-done((f32[16,256]{1,0:T(8,128)S(1)}, f32[16,256]{1,0:T(8,128)S(1)}, u32[]{:S(2)}, u32[]{:S(2)}) %collective-permute-start.12) | collective-permute-done | bytes 16416 | tf_op jit(solution)/shard_map/ppermute | solution.py:23
  94.3 0.1 fusion.197
  94.9 0.1 multiply_multiply_fusion.13
  95.1 0.1 multiply_multiply_fusion.12
  95.4 0.1 multiply_multiply_fusion.11
  98.6 1.9 %collective-permute-start.14 = (f32[3,32,256]{2,1,0:T(8,128)S(1)}, f32[3,32,256]{2,1,0:T(8,128)S(1)}, u32[]{:S(2)}, u32[]{:S(2)}) collective-permute-start(f32[3,32,256]{2,1,0:T(8,128)S(1)} %pad_maximum_fusion.2), channel_id=1, source_target_pairs={{0,8},{8,16},{16,24},{24,32},{32,40},{40,48},{48,56},{56,64},{64,7... | collective-permute-start | bytes 294920 | tf_op jit(solution)/shard_map/ppermute | solution.py:68
  100.6 1.9 %collective-permute-start.17 = (f32[2,32,256]{2,1,0:T(8,128)S(1)}, f32[2,32,256]{2,1,0:T(8,128)S(1)}, u32[]{:S(2)}, u32[]{:S(2)}) collective-permute-start(f32[2,32,256]{2,1,0:T(8,128)S(1)} %pad_maximum_fusion.7), channel_id=1, source_target_pairs={{0,32},{8,40},{16,48},{24,56},{32,64},{40,72},{48,80},{56,88},{64,... | collective-permute-start | bytes 196616 | tf_op jit(solution)/shard_map/ppermute | solution.py:68
  102.5 4.3 %collective-permute-start.16 = (f32[2,32,256]{2,1,0:T(8,128)S(1)}, f32[2,32,256]{2,1,0:T(8,128)S(1)}, u32[]{:S(2)}, u32[]{:S(2)}) collective-permute-start(f32[2,32,256]{2,1,0:T(8,128)S(1)} %pad_maximum_fusion.7), channel_id=1, source_target_pairs={{0,24},{8,32},{16,40},{24,48},{32,56},{40,64},{48,72},{56,80},{64,... | collective-permute-start | bytes 196616 | tf_op jit(solution)/shard_map/ppermute | solution.py:68
  106.8 5.2 %collective-permute-start.15 = (f32[2,32,256]{2,1,0:T(8,128)S(1)}, f32[2,32,256]{2,1,0:T(8,128)S(1)}, u32[]{:S(2)}, u32[]{:S(2)}) collective-permute-start(f32[2,32,256]{2,1,0:T(8,128)S(1)} %pad_maximum_fusion.7), channel_id=1, source_target_pairs={{0,16},{8,24},{16,32},{24,40},{32,48},{40,56},{48,64},{56,72},{64,... | collective-permute-start | bytes 196616 | tf_op jit(solution)/shard_map/ppermute | solution.py:68
  112.1 4.5 %collective-permute-done.15 = f32[2,32,256]{2,1,0:T(8,128)S(1)} collective-permute-done((f32[2,32,256]{2,1,0:T(8,128)S(1)}, f32[2,32,256]{2,1,0:T(8,128)S(1)}, u32[]{:S(2)}, u32[]{:S(2)}) %collective-permute-start.15) | collective-permute-done | bytes 65568 | tf_op jit(solution)/shard_map/ppermute | solution.py:68
  116.7 6.8 %collective-permute-start.20 = (f32[2,32,256]{2,1,0:T(8,128)S(1)}, f32[2,32,256]{2,1,0:T(8,128)S(1)}, u32[]{:S(2)}, u32[]{:S(2)}) collective-permute-start(f32[2,32,256]{2,1,0:T(8,128)S(1)} %pad_maximum_fusion.8), channel_id=1, source_target_pairs={{0,96},{8,104},{16,112},{24,120},{32,128},{40,136},{48,144},{56,15... | collective-permute-start | bytes 196616 | tf_op jit(solution)/shard_map/ppermute | solution.py:68
  123.5 3.7 %collective-permute-start.19 = (f32[2,32,256]{2,1,0:T(8,128)S(1)}, f32[2,32,256]{2,1,0:T(8,128)S(1)}, u32[]{:S(2)}, u32[]{:S(2)}) collective-permute-start(f32[2,32,256]{2,1,0:T(8,128)S(1)} %pad_maximum_fusion.8), channel_id=1, source_target_pairs={{0,64},{8,72},{16,80},{24,88},{32,96},{40,104},{48,112},{56,120},{... | collective-permute-start | bytes 196616 | tf_op jit(solution)/shard_map/ppermute | solution.py:68
  127.2 3.2 %collective-permute-start.18 = (f32[2,32,256]{2,1,0:T(8,128)S(1)}, f32[2,32,256]{2,1,0:T(8,128)S(1)}, u32[]{:S(2)}, u32[]{:S(2)}) collective-permute-start(f32[2,32,256]{2,1,0:T(8,128)S(1)} %pad_maximum_fusion.8), channel_id=1, source_target_pairs={{0,32},{8,40},{16,48},{24,56},{32,64},{40,72},{48,80},{56,88},{64,... | collective-permute-start | bytes 196616 | tf_op jit(solution)/shard_map/ppermute | solution.py:68
  130.5 2.2 %collective-permute-done.19 = f32[2,32,256]{2,1,0:T(8,128)S(1)} collective-permute-done((f32[2,32,256]{2,1,0:T(8,128)S(1)}, f32[2,32,256]{2,1,0:T(8,128)S(1)}, u32[]{:S(2)}, u32[]{:S(2)}) %collective-permute-start.19) | collective-permute-done | bytes 65568 | tf_op jit(solution)/shard_map/ppermute | solution.py:68
  132.7 2.0 %collective-permute-done.18 = f32[2,32,256]{2,1,0:T(8,128)S(1)} collective-permute-done((f32[2,32,256]{2,1,0:T(8,128)S(1)}, f32[2,32,256]{2,1,0:T(8,128)S(1)}, u32[]{:S(2)}, u32[]{:S(2)}) %collective-permute-start.18) | collective-permute-done | bytes 65568 | tf_op jit(solution)/shard_map/ppermute | solution.py:68
  134.7 4.6 %collective-permute-start.21 = (f32[2,32,256]{2,1,0:T(8,128)S(1)}, f32[2,32,256]{2,1,0:T(8,128)S(1)}, u32[]{:S(2)}, u32[]{:S(2)}) collective-permute-start(f32[2,32,256]{2,1,0:T(8,128)S(1)} %pad_maximum_fusion.9), channel_id=1, source_target_pairs={{0,128},{8,136},{16,144},{24,152},{32,160},{40,168},{48,176},{56,1... | collective-permute-start | bytes 196616 | tf_op jit(solution)/shard_map/ppermute | solution.py:68
  139.3 7.6 %collective-permute-start.22 = (f32[2,32,256]{2,1,0:T(8,128)S(1)}, f32[2,32,256]{2,1,0:T(8,128)S(1)}, u32[]{:S(2)}, u32[]{:S(2)}) collective-permute-start(f32[2,32,256]{2,1,0:T(8,128)S(1)} %pad_maximum_fusion.9), channel_id=1, source_target_pairs={{0,256},{8,264},{16,272},{24,280},{32,288},{40,296},{48,304},{56,3... | collective-permute-start | bytes 196616 | tf_op jit(solution)/shard_map/ppermute | solution.py:68
  146.9 4.5 %collective-permute-start.23 = (f32[2,32,256]{2,1,0:T(8,128)S(1)}, f32[2,32,256]{2,1,0:T(8,128)S(1)}, u32[]{:S(2)}, u32[]{:S(2)}) collective-permute-start(f32[2,32,256]{2,1,0:T(8,128)S(1)} %pad_maximum_fusion.9), channel_id=1, source_target_pairs={{0,384},{8,392},{16,400},{24,408},{32,416},{40,424},{48,432},{56,4... | collective-permute-start | bytes 196616 | tf_op jit(solution)/shard_map/ppermute | solution.py:68
  151.4 3.5 %collective-permute-done.22 = f32[2,32,256]{2,1,0:T(8,128)S(1)} collective-permute-done((f32[2,32,256]{2,1,0:T(8,128)S(1)}, f32[2,32,256]{2,1,0:T(8,128)S(1)}, u32[]{:S(2)}, u32[]{:S(2)}) %collective-permute-start.22) | collective-permute-done | bytes 65568 | tf_op jit(solution)/shard_map/ppermute | solution.py:68
  154.9 4.5 %collective-permute-done.23 = f32[2,32,256]{2,1,0:T(8,128)S(1)} collective-permute-done((f32[2,32,256]{2,1,0:T(8,128)S(1)}, f32[2,32,256]{2,1,0:T(8,128)S(1)}, u32[]{:S(2)}, u32[]{:S(2)}) %collective-permute-start.23) | collective-permute-done | bytes 65568 | tf_op jit(solution)/shard_map/ppermute | solution.py:68
  159.4 0.6 slice_subtract_fusion.2
  (128 shorter events, 7.3 us)
Async XLA Ops:
  0.6 0.8 copy-start
  2.3 9.7 %collective-permute-start.1 = (f32[4,16,256]{2,1,0:T(8,128)S(1)}, f32[4,16,256]{2,1,0:T(8,128)S(1)}, u32[]{:S(2)}, u32[]{:S(2)}) collective-permute-start(f32[4,16,256]{2,1,0:T(8,128)S(1)} %get-tuple-element.42), channel_id=1, source_target_pairs={{1,0},{2,1},{3,2},{4,3},{5,4},{6,5},{7,6},{9,8},{10,9},{11,10},{12... | collective-permute-start | bytes 196616 | tf_op jit(solution)/shard_map/ppermute | solution.py:24
  6.8 8.3 %collective-permute-start = (f32[4,16,256]{2,1,0:T(8,128)S(1)}, f32[4,16,256]{2,1,0:T(8,128)S(1)}, u32[]{:S(2)}, u32[]{:S(2)}) collective-permute-start(f32[4,16,256]{2,1,0:T(8,128)S(1)} %get-tuple-element.41), channel_id=1, source_target_pairs={{0,1},{1,2},{2,3},{3,4},{4,5},{5,6},{6,7},{8,9},{9,10},{10,11},{11... | collective-permute-start | bytes 196616 | tf_op jit(solution)/shard_map/ppermute | solution.py:23
  9.6 5.6 %copy-start.1 = (f32[2,32,256]{2,1,0:T(8,128)S(1)}, f32[2,32,256]{2,1,0:T(8,128)}, u32[]{:S(2)}) copy-start(f32[2,32,256]{2,1,0:T(8,128)} %param.6) | copy-start | bytes 196612
  19.6 14.0 %collective-permute-start.5 = (f32[2,32,256]{2,1,0:T(8,128)S(1)}, f32[2,32,256]{2,1,0:T(8,128)S(1)}, u32[]{:S(2)}, u32[]{:S(2)}) collective-permute-start(f32[2,32,256]{2,1,0:T(8,128)S(1)} %pad_maximum_fusion.3), channel_id=1, source_target_pairs={{0,32},{8,40},{16,48},{24,56},{32,64},{40,72},{48,80},{56,88},{64,... | collective-permute-start | bytes 196616 | tf_op jit(solution)/shard_map/ppermute | solution.py:68
  23.4 10.2 %collective-permute-start.4 = (f32[2,32,256]{2,1,0:T(8,128)S(1)}, f32[2,32,256]{2,1,0:T(8,128)S(1)}, u32[]{:S(2)}, u32[]{:S(2)}) collective-permute-start(f32[2,32,256]{2,1,0:T(8,128)S(1)} %pad_maximum_fusion.3), channel_id=1, source_target_pairs={{0,24},{8,32},{16,40},{24,48},{32,56},{40,64},{48,72},{56,80},{64,... | collective-permute-start | bytes 196616 | tf_op jit(solution)/shard_map/ppermute | solution.py:68
  25.6 14.1 %collective-permute-start.3 = (f32[2,32,256]{2,1,0:T(8,128)S(1)}, f32[2,32,256]{2,1,0:T(8,128)S(1)}, u32[]{:S(2)}, u32[]{:S(2)}) collective-permute-start(f32[2,32,256]{2,1,0:T(8,128)S(1)} %pad_maximum_fusion.3), channel_id=1, source_target_pairs={{0,16},{8,24},{16,32},{24,40},{32,48},{40,56},{48,64},{56,72},{64,... | collective-permute-start | bytes 196616 | tf_op jit(solution)/shard_map/ppermute | solution.py:68
  29.9 9.9 %collective-permute-start.2 = (f32[2,32,256]{2,1,0:T(8,128)S(1)}, f32[2,32,256]{2,1,0:T(8,128)S(1)}, u32[]{:S(2)}, u32[]{:S(2)}) collective-permute-start(f32[2,32,256]{2,1,0:T(8,128)S(1)} %pad_maximum_fusion.3), channel_id=1, source_target_pairs={{0,8},{8,16},{16,24},{24,32},{32,40},{40,48},{48,56},{56,64},{64,7... | collective-permute-start | bytes 196616 | tf_op jit(solution)/shard_map/ppermute | solution.py:68
  39.8 16.1 %collective-permute-start.8 = (f32[2,32,256]{2,1,0:T(8,128)S(1)}, f32[2,32,256]{2,1,0:T(8,128)S(1)}, u32[]{:S(2)}, u32[]{:S(2)}) collective-permute-start(f32[2,32,256]{2,1,0:T(8,128)S(1)} %pad_maximum_fusion.4), channel_id=1, source_target_pairs={{0,96},{8,104},{16,112},{24,120},{32,128},{40,136},{48,144},{56,15... | collective-permute-start | bytes 196616 | tf_op jit(solution)/shard_map/ppermute | solution.py:68
  45.6 10.2 %collective-permute-start.7 = (f32[2,32,256]{2,1,0:T(8,128)S(1)}, f32[2,32,256]{2,1,0:T(8,128)S(1)}, u32[]{:S(2)}, u32[]{:S(2)}) collective-permute-start(f32[2,32,256]{2,1,0:T(8,128)S(1)} %pad_maximum_fusion.4), channel_id=1, source_target_pairs={{0,64},{8,72},{16,80},{24,88},{32,96},{40,104},{48,112},{56,120},{... | collective-permute-start | bytes 196616 | tf_op jit(solution)/shard_map/ppermute | solution.py:68
  50.8 7.4 %collective-permute-start.6 = (f32[2,32,256]{2,1,0:T(8,128)S(1)}, f32[2,32,256]{2,1,0:T(8,128)S(1)}, u32[]{:S(2)}, u32[]{:S(2)}) collective-permute-start(f32[2,32,256]{2,1,0:T(8,128)S(1)} %pad_maximum_fusion.4), channel_id=1, source_target_pairs={{0,32},{8,40},{16,48},{24,56},{32,64},{40,72},{48,80},{56,88},{64,... | collective-permute-start | bytes 196616 | tf_op jit(solution)/shard_map/ppermute | solution.py:68
  58.2 19.1 %collective-permute-start.9 = (f32[2,32,256]{2,1,0:T(8,128)S(1)}, f32[2,32,256]{2,1,0:T(8,128)S(1)}, u32[]{:S(2)}, u32[]{:S(2)}) collective-permute-start(f32[2,32,256]{2,1,0:T(8,128)S(1)} %pad_maximum_fusion.5), channel_id=1, source_target_pairs={{0,128},{8,136},{16,144},{24,152},{32,160},{40,168},{48,176},{56,1... | collective-permute-start | bytes 196616 | tf_op jit(solution)/shard_map/ppermute | solution.py:68
  65.7 16.2 %collective-permute-start.10 = (f32[2,32,256]{2,1,0:T(8,128)S(1)}, f32[2,32,256]{2,1,0:T(8,128)S(1)}, u32[]{:S(2)}, u32[]{:S(2)}) collective-permute-start(f32[2,32,256]{2,1,0:T(8,128)S(1)} %pad_maximum_fusion.5), channel_id=1, source_target_pairs={{0,256},{8,264},{16,272},{24,280},{32,288},{40,296},{48,304},{56,3... | collective-permute-start | bytes 196616 | tf_op jit(solution)/shard_map/ppermute | solution.py:68
  69.7 13.7 %collective-permute-start.11 = (f32[2,32,256]{2,1,0:T(8,128)S(1)}, f32[2,32,256]{2,1,0:T(8,128)S(1)}, u32[]{:S(2)}, u32[]{:S(2)}) collective-permute-start(f32[2,32,256]{2,1,0:T(8,128)S(1)} %pad_maximum_fusion.5), channel_id=1, source_target_pairs={{0,384},{8,392},{16,400},{24,408},{32,416},{40,424},{48,432},{56,4... | collective-permute-start | bytes 196616 | tf_op jit(solution)/shard_map/ppermute | solution.py:68
  83.4 5.9 %collective-permute-start.13 = (f32[16,256]{1,0:T(8,128)S(1)}, f32[16,256]{1,0:T(8,128)S(1)}, u32[]{:S(2)}, u32[]{:S(2)}) collective-permute-start(f32[16,256]{1,0:T(8,128)S(1)} %get-tuple-element.62), channel_id=1, source_target_pairs={{1,0},{2,1},{3,2},{4,3},{5,4},{6,5},{7,6},{9,8},{10,9},{11,10},{12... | collective-permute-start | bytes 49160 | tf_op jit(solution)/shard_map/ppermute | solution.py:24
  86.6 7.7 %collective-permute-start.12 = (f32[16,256]{1,0:T(8,128)S(1)}, f32[16,256]{1,0:T(8,128)S(1)}, u32[]{:S(2)}, u32[]{:S(2)}) collective-permute-start(f32[16,256]{1,0:T(8,128)S(1)} %get-tuple-element.61), channel_id=1, source_target_pairs={{0,1},{1,2},{2,3},{3,4},{4,5},{5,6},{6,7},{8,9},{9,10},{10,11},{11... | collective-permute-start | bytes 49160 | tf_op jit(solution)/shard_map/ppermute | solution.py:23
  98.6 18.0 %collective-permute-start.14 = (f32[3,32,256]{2,1,0:T(8,128)S(1)}, f32[3,32,256]{2,1,0:T(8,128)S(1)}, u32[]{:S(2)}, u32[]{:S(2)}) collective-permute-start(f32[3,32,256]{2,1,0:T(8,128)S(1)} %pad_maximum_fusion.2), channel_id=1, source_target_pairs={{0,8},{8,16},{16,24},{24,32},{32,40},{40,48},{48,56},{56,64},{64,7... | collective-permute-start | bytes 294920 | tf_op jit(solution)/shard_map/ppermute | solution.py:68
  100.6 11.5 %collective-permute-start.17 = (f32[2,32,256]{2,1,0:T(8,128)S(1)}, f32[2,32,256]{2,1,0:T(8,128)S(1)}, u32[]{:S(2)}, u32[]{:S(2)}) collective-permute-start(f32[2,32,256]{2,1,0:T(8,128)S(1)} %pad_maximum_fusion.7), channel_id=1, source_target_pairs={{0,32},{8,40},{16,48},{24,56},{32,64},{40,72},{48,80},{56,88},{64,... | collective-permute-start | bytes 196616 | tf_op jit(solution)/shard_map/ppermute | solution.py:68
  102.5 9.6 %collective-permute-start.16 = (f32[2,32,256]{2,1,0:T(8,128)S(1)}, f32[2,32,256]{2,1,0:T(8,128)S(1)}, u32[]{:S(2)}, u32[]{:S(2)}) collective-permute-start(f32[2,32,256]{2,1,0:T(8,128)S(1)} %pad_maximum_fusion.7), channel_id=1, source_target_pairs={{0,24},{8,32},{16,40},{24,48},{32,56},{40,64},{48,72},{56,80},{64,... | collective-permute-start | bytes 196616 | tf_op jit(solution)/shard_map/ppermute | solution.py:68
  106.8 9.8 %collective-permute-start.15 = (f32[2,32,256]{2,1,0:T(8,128)S(1)}, f32[2,32,256]{2,1,0:T(8,128)S(1)}, u32[]{:S(2)}, u32[]{:S(2)}) collective-permute-start(f32[2,32,256]{2,1,0:T(8,128)S(1)} %pad_maximum_fusion.7), channel_id=1, source_target_pairs={{0,16},{8,24},{16,32},{24,40},{32,48},{40,56},{48,64},{56,72},{64,... | collective-permute-start | bytes 196616 | tf_op jit(solution)/shard_map/ppermute | solution.py:68
  116.7 13.8 %collective-permute-start.20 = (f32[2,32,256]{2,1,0:T(8,128)S(1)}, f32[2,32,256]{2,1,0:T(8,128)S(1)}, u32[]{:S(2)}, u32[]{:S(2)}) collective-permute-start(f32[2,32,256]{2,1,0:T(8,128)S(1)} %pad_maximum_fusion.8), channel_id=1, source_target_pairs={{0,96},{8,104},{16,112},{24,120},{32,128},{40,136},{48,144},{56,15... | collective-permute-start | bytes 196616 | tf_op jit(solution)/shard_map/ppermute | solution.py:68
  123.5 9.2 %collective-permute-start.19 = (f32[2,32,256]{2,1,0:T(8,128)S(1)}, f32[2,32,256]{2,1,0:T(8,128)S(1)}, u32[]{:S(2)}, u32[]{:S(2)}) collective-permute-start(f32[2,32,256]{2,1,0:T(8,128)S(1)} %pad_maximum_fusion.8), channel_id=1, source_target_pairs={{0,64},{8,72},{16,80},{24,88},{32,96},{40,104},{48,112},{56,120},{... | collective-permute-start | bytes 196616 | tf_op jit(solution)/shard_map/ppermute | solution.py:68
  127.2 7.4 %collective-permute-start.18 = (f32[2,32,256]{2,1,0:T(8,128)S(1)}, f32[2,32,256]{2,1,0:T(8,128)S(1)}, u32[]{:S(2)}, u32[]{:S(2)}) collective-permute-start(f32[2,32,256]{2,1,0:T(8,128)S(1)} %pad_maximum_fusion.8), channel_id=1, source_target_pairs={{0,32},{8,40},{16,48},{24,56},{32,64},{40,72},{48,80},{56,88},{64,... | collective-permute-start | bytes 196616 | tf_op jit(solution)/shard_map/ppermute | solution.py:68
  134.7 16.7 %collective-permute-start.21 = (f32[2,32,256]{2,1,0:T(8,128)S(1)}, f32[2,32,256]{2,1,0:T(8,128)S(1)}, u32[]{:S(2)}, u32[]{:S(2)}) collective-permute-start(f32[2,32,256]{2,1,0:T(8,128)S(1)} %pad_maximum_fusion.9), channel_id=1, source_target_pairs={{0,128},{8,136},{16,144},{24,152},{32,160},{40,168},{48,176},{56,1... | collective-permute-start | bytes 196616 | tf_op jit(solution)/shard_map/ppermute | solution.py:68
  139.3 15.6 %collective-permute-start.22 = (f32[2,32,256]{2,1,0:T(8,128)S(1)}, f32[2,32,256]{2,1,0:T(8,128)S(1)}, u32[]{:S(2)}, u32[]{:S(2)}) collective-permute-start(f32[2,32,256]{2,1,0:T(8,128)S(1)} %pad_maximum_fusion.9), channel_id=1, source_target_pairs={{0,256},{8,264},{16,272},{24,280},{32,288},{40,296},{48,304},{56,3... | collective-permute-start | bytes 196616 | tf_op jit(solution)/shard_map/ppermute | solution.py:68
  146.9 12.5 %collective-permute-start.23 = (f32[2,32,256]{2,1,0:T(8,128)S(1)}, f32[2,32,256]{2,1,0:T(8,128)S(1)}, u32[]{:S(2)}, u32[]{:S(2)}) collective-permute-start(f32[2,32,256]{2,1,0:T(8,128)S(1)} %pad_maximum_fusion.9), channel_id=1, source_target_pairs={{0,384},{8,392},{16,400},{24,408},{32,416},{40,424},{48,432},{56,4... | collective-permute-start | bytes 196616 | tf_op jit(solution)/shard_map/ppermute | solution.py:68

commit v2 on v1

--- a/solution.py
+++ b/solution.py
@@ -86,6 +86,36 @@
     return window[1], (carried[0] if extra else None)
 
 
+def shift_down(x, by, fill):
+    head = jnp.full(x.shape[:1] + (by,) + x.shape[2:], fill, x.dtype)
+    return jnp.concatenate([head, x[:, : x.shape[1] - by]], axis=1)
+
+
+def transposed_states(decay, offset, extra):
+    count = lax.axis_size("tm")
+    rows, cols = decay.shape
+    parts = jnp.stack([decay, offset] + extra).reshape(2 + len(extra), count, rows * cols // count)
+    cells = lax.all_to_all(parts, "tm", 1, 1, tiled=True)
+    factor, shift = cells[0], cells[1]
+    span = 1
+    while span < count:
+        earlier_factor = shift_down(factor[None], span, 1.0)[0]
+        earlier_shift = shift_down(shift[None], span, 0.0)[0]
+        factor, shift = factor * earlier_factor, factor * earlier_shift + shift
+        span *= 2
+    closing = shift[count - 1 :]
+    before_factor = shift_down(factor[None], 1, 1.0)[0]
+    before_shift = shift_down(shift[None], 1, 0.0)[0]
+    states = before_factor * closing + before_shift
+    outs = [states]
+    if extra:
+        ends = cells[2]
+        outs.append(jnp.concatenate([ends[count - 1 :], ends[: count - 1]], axis=0) - states)
+    back = lax.all_to_all(jnp.stack(outs), "tm", 1, 1, tiled=True)
+    back = back.reshape(len(outs), rows, cols)
+    return back[0], (back[1:] if extra else None)
+
+
 def on_device(start_states, region_map, source, front):
     field_now = start_states[0]
     rows, cols = field_now.shape
@@ -130,9 +160,8 @@
         decay = jnp.where(keep_map, decay, 0.0)
         offset = fine_end - decay * field_now
         last = sweep == ITERS - 1
-        field_now, previous_end = periodic_states(decay, offset, [fine_end] if last else [])
-    jumps = previous_end[0] - field_now
-    return (field_now[None], jumps[None])
+        field_now, jumps = transposed_states(decay, offset, [fine_end] if last else [])
+    return (field_now[None], jumps)
 
 
 def solution(mesh):

time: 161 us -> 135 us (0.84)
  the two profiles are of different devices: /device:TPU:8 before, /device:TPU:7 now
where the time goes in v2:
time: 135 us
  blocking collectives  97.4 us (72%)
  starting transfers between devices  13.5 us (10%)
  other arithmetic  11.6 us (9%)
  between operations  4.82 us (4%)
  waiting for transfers between devices  4.64 us (3%)
  local copies, waits for them, and re-layouts  2.72 us (2%)
    all_to_all x2, blocking collectives, transposed_states(): cells = lax.all_to_all(parts, 'tm', 1, 1, tiled=True)  59.2 us
    all_to_all x2, blocking collectives, transposed_states(): back = lax.all_to_all(jnp.stack(outs), 'tm', 1, 1, tiled=True)  38.2 us
    ppermute x2, starting transfers between devices, with_halo(): lax.ppermute(lax.slice_in_dim(block, rows - width, rows, axis=block.ndim...  9.11 us
    ppermute x2, waiting for transfers between devices, with_halo(): lax.ppermute(lax.slice_in_dim(block, 0, width, axis=block.ndim - 2), 'spa...  4.63 us
    ppermute x2, starting transfers between devices, with_halo(): lax.ppermute(lax.slice_in_dim(block, 0, width, axis=block.ndim - 2), 'spa...  4.38 us
    mul x32, other arithmetic, flux_terms(): col_flux = col_w * col_diff  3.56 us
    add x29, other arithmetic, single_step(): return (values + mobile_ext * (divergence + current), diagonal)  2.76 us
  transfers between devices with their start and end apart: 4, of which 1 were waited for; matrix products, arithmetic and copies ran while one was open for 1% of the time, Pallas kernels for 0%

profile of v2, /device:TPU:7, one launch (start us, length us, event | category | flops | bytes accessed | tf_op | source)
XLA Modules:
  0.0 134.6 jit_solution(2252772722916426609)
XLA Ops:
  0.6 0.8 add_bitcast_fusion.3
  1.4 0.8 pad_maximum_fusion.1
  2.3 2.5 %collective-permute-start.1 = (f32[4,16,256]{2,1,0:T(8,128)S(1)}, f32[4,16,256]{2,1,0:T(8,128)S(1)}, u32[]{:S(2)}, u32[]{:S(2)}) collective-permute-start(f32[4,16,256]{2,1,0:T(8,128)S(1)} %get-tuple-element.61), channel_id=1, source_target_pairs={{1,0},{2,1},{3,2},{4,3},{5,4},{6,5},{7,6},{9,8},{10,9},{11,10},{12... | collective-permute-start | bytes 196616 | tf_op jit(solution)/shard_map/ppermute | solution.py:24
  4.7 4.9 %collective-permute-start = (f32[4,16,256]{2,1,0:T(8,128)S(1)}, f32[4,16,256]{2,1,0:T(8,128)S(1)}, u32[]{:S(2)}, u32[]{:S(2)}) collective-permute-start(f32[4,16,256]{2,1,0:T(8,128)S(1)} %get-tuple-element.60), channel_id=1, source_target_pairs={{0,1},{1,2},{2,3},{3,4},{4,5},{5,6},{6,7},{8,9},{9,10},{10,11},{11... | collective-permute-start | bytes 196616 | tf_op jit(solution)/shard_map/ppermute | solution.py:23
  13.1 0.2 fusion.173
  13.3 0.1 fusion.185
  13.7 0.1 multiply_multiply_fusion.28
  13.9 0.1 multiply_multiply_fusion.27
  14.2 0.1 multiply_multiply_fusion.26
  14.4 0.1 multiply_multiply_fusion.25
  14.7 0.1 multiply_multiply_fusion.24
  14.9 0.1 multiply_multiply_fusion.23
  15.2 0.1 multiply_multiply_fusion.22
  15.5 0.1 multiply_multiply_fusion.21
  15.7 0.1 multiply_multiply_fusion.20
  16.0 0.1 multiply_multiply_fusion.19
  16.2 0.1 multiply_multiply_fusion.18
  16.5 0.1 multiply_multiply_fusion.17
  16.8 0.1 multiply_multiply_fusion.16
  17.0 0.1 multiply_multiply_fusion.15
  17.5 35.2 %all_to_all.20 = f32[2,64,128]{2,0,1:T(2,128)S(1)} all-to-all(f32[2,64,128]{2,0,1:T(2,128)S(1)} %pad_maximum_fusion.3), channel_id=1, replica_groups=mesh['tm'=64,'space'=8] {'tm'}, dimensions={1} | all-to-all | bytes 131072 | tf_op jit(solution)/shard_map/all_to_all | solution.py:98
  53.5 18.4 %all_to_all.21 = f32[1,64,128]{2,0,1:T(1,128)S(1)} all-to-all(f32[1,64,128]{2,0,1:T(1,128)S(1)} %pad_add_fusion.1), channel_id=1, replica_groups=mesh['tm'=64,'space'=8] {'tm'}, dimensions={1} | all-to-all | bytes 65536 | tf_op jit(solution)/shard_map/all_to_all | solution.py:114
  72.1 4.2 %collective-permute-start.2 = (f32[16,256]{1,0:T(8,128)S(1)}, f32[16,256]{1,0:T(8,128)S(1)}, u32[]{:S(2)}, u32[]{:S(2)}) collective-permute-start(f32[16,256]{1,0:T(8,128)S(1)} %slice.1160), channel_id=1, source_target_pairs={{0,1},{1,2},{2,3},{3,4},{4,5},{5,6},{6,7},{8,9},{9,10},{10,11},{11... | collective-permute-start | bytes 49160 | tf_op jit(solution)/shard_map/ppermute | solution.py:23
  76.2 0.5 broadcast.455
  76.8 0.7 reduce.19
  77.5 1.9 %collective-permute-start.3 = (f32[16,256]{1,0:T(8,128)S(1)}, f32[16,256]{1,0:T(8,128)S(1)}, u32[]{:S(2)}, u32[]{:S(2)}) collective-permute-start(f32[16,256]{1,0:T(8,128)S(1)} %slice.1162), channel_id=1, source_target_pairs={{1,0},{2,1},{3,2},{4,3},{5,4},{6,5},{7,6},{9,8},{10,9},{11,10},{12... | collective-permute-start | bytes 49160 | tf_op jit(solution)/shard_map/ppermute | solution.py:24
  79.5 4.6 %collective-permute-done.3 = f32[16,256]{1,0:T(8,128)S(1)} collective-permute-done((f32[16,256]{1,0:T(8,128)S(1)}, f32[16,256]{1,0:T(8,128)S(1)}, u32[]{:S(2)}, u32[]{:S(2)}) %collective-permute-start.3) | collective-permute-done | bytes 16416 | tf_op jit(solution)/shard_map/ppermute | solution.py:24
  84.1 0.1 fusion.172
  84.4 0.1 multiply_multiply_fusion.14
  84.6 0.1 multiply_multiply_fusion.13
  84.9 0.1 multiply_multiply_fusion.12
  85.1 0.1 multiply_multiply_fusion.11
  85.4 0.1 multiply_multiply_fusion.10
  85.7 0.1 multiply_multiply_fusion.9
  85.9 0.1 multiply_multiply_fusion.8
  86.2 0.1 multiply_multiply_fusion.7
  86.4 0.1 multiply_multiply_fusion.6
  86.7 0.1 multiply_multiply_fusion.5
  87.0 0.1 multiply_multiply_fusion.4
  87.2 0.1 multiply_multiply_fusion.3
  87.5 0.1 multiply_multiply_fusion.2
  87.7 0.1 multiply_multiply_fusion.1
  88.0 0.1 multiply_multiply_fusion
  88.6 24.0 %all_to_all.22 = f32[3,64,128]{2,0,1:T(4,128)S(1)} all-to-all(f32[3,64,128]{2,0,1:T(4,128)S(1)} %pad_maximum_fusion.2), channel_id=1, replica_groups=mesh['tm'=64,'space'=8] {'tm'}, dimensions={1} | all-to-all | bytes 196608 | tf_op jit(solution)/shard_map/all_to_all | solution.py:98
  113.5 19.7 %all_to_all.23 = f32[2,64,128]{2,0,1:T(2,128)S(1)} all-to-all(f32[2,64,128]{2,0,1:T(2,128)S(1)} %pad_maximum_fusion.4), channel_id=1, replica_groups=mesh['tm'=64,'space'=8] {'tm'}, dimensions={1} | all-to-all | bytes 131072 | tf_op jit(solution)/shard_map/all_to_all | solution.py:114
  133.2 0.2 slice_reduce_fusion
  133.4 0.6 slice.1317
  134.0 0.6 slice.1319
  (140 shorter events, 6.5 us)
Async XLA Ops:
  0.6 0.8 copy-start
  2.3 10.6 %collective-permute-start.1 = (f32[4,16,256]{2,1,0:T(8,128)S(1)}, f32[4,16,256]{2,1,0:T(8,128)S(1)}, u32[]{:S(2)}, u32[]{:S(2)}) collective-permute-start(f32[4,16,256]{2,1,0:T(8,128)S(1)} %get-tuple-element.61), channel_id=1, source_target_pairs={{1,0},{2,1},{3,2},{4,3},{5,4},{6,5},{7,6},{9,8},{10,9},{11,10},{12... | collective-permute-start | bytes 196616 | tf_op jit(solution)/shard_map/ppermute | solution.py:24
  4.7 8.1 %collective-permute-start = (f32[4,16,256]{2,1,0:T(8,128)S(1)}, f32[4,16,256]{2,1,0:T(8,128)S(1)}, u32[]{:S(2)}, u32[]{:S(2)}) collective-permute-start(f32[4,16,256]{2,1,0:T(8,128)S(1)} %get-tuple-element.60), channel_id=1, source_target_pairs={{0,1},{1,2},{2,3},{3,4},{4,5},{5,6},{6,7},{8,9},{9,10},{10,11},{11... | collective-permute-start | bytes 196616 | tf_op jit(solution)/shard_map/ppermute | solution.py:23
  10.5 2.4 %copy-start.1 = (f32[2,32,256]{2,1,0:T(8,128)S(1)}, f32[2,32,256]{2,1,0:T(8,128)}, u32[]{:S(2)}) copy-start(f32[2,32,256]{2,1,0:T(8,128)} %param.6) | copy-start | bytes 196612
  72.1 7.4 %collective-permute-start.2 = (f32[16,256]{1,0:T(8,128)S(1)}, f32[16,256]{1,0:T(8,128)S(1)}, u32[]{:S(2)}, u32[]{:S(2)}) collective-permute-start(f32[16,256]{1,0:T(8,128)S(1)} %slice.1160), channel_id=1, source_target_pairs={{0,1},{1,2},{2,3},{3,4},{4,5},{5,6},{6,7},{8,9},{9,10},{10,11},{11... | collective-permute-start | bytes 49160 | tf_op jit(solution)/shard_map/ppermute | solution.py:23
  77.5 6.6 %collective-permute-start.3 = (f32[16,256]{1,0:T(8,128)S(1)}, f32[16,256]{1,0:T(8,128)S(1)}, u32[]{:S(2)}, u32[]{:S(2)}) collective-permute-start(f32[16,256]{1,0:T(8,128)S(1)} %slice.1162), channel_id=1, source_target_pairs={{1,0},{2,1},{3,2},{4,3},{5,4},{6,5},{7,6},{9,8},{10,9},{11,10},{12... | collective-permute-start | bytes 49160 | tf_op jit(solution)/shard_map/ppermute | solution.py:24

commit v3 on v2

--- a/solution.py
+++ b/solution.py
@@ -120,6 +120,7 @@
     field_now = start_states[0]
     rows, cols = field_now.shape
     width = FINE
+    reach = ITERS * FINE if ITERS * FINE <= rows else FINE
     slices = lax.axis_size("tm")
     slice_index = lax.axis_index("tm")
     scale = 2.0 * math.pi / (slices * FINE)
@@ -127,40 +128,55 @@
     stacked = jnp.stack(
         [field_now, region_map.astype(jnp.float32) + 1.0, source[0], source[1]], 0
     )
-    extended = with_halo(stacked, width)
+    extended = with_halo(stacked, reach)
     code = extended[1]
     reluct = lookup_shifted(code, RELUCTIVITY)
     satur = lookup_shifted(code, SATURATION)
-    mobile_ext = lookup_shifted(code, MOBILITY)
-    src_cos, src_sin = extended[2], extended[3]
-    row_rel = face_terms(reluct, 0)
-    row_sat = face_terms(satur, 0)
-    col_rel = face_terms(reluct, 1)
-    col_sat = face_terms(satur, 1)
-    mobile = mobile_ext[width : width + rows]
-
-    def single_step(values, step_index):
-        divergence, diagonal = flux_terms(values, row_rel, row_sat, col_rel, col_sat)
-        phase_angle = (slice_index * FINE + step_index).astype(jnp.float32) * scale
-        current = src_cos * jnp.cos(phase_angle) + src_sin * jnp.sin(phase_angle)
-        return values + mobile_ext * (divergence + current), diagonal
-
+    mobile_all = lookup_shifted(code, MOBILITY)
+    cos_all, sin_all = extended[2], extended[3]
     cut_slice = (front - 1) % slices
     keep_map = slice_index != cut_slice
-    values_ext = extended[0]
-    for sweep in range(ITERS):
-        if sweep > 0:
-            values_ext = with_halo(field_now, width)
-        fine_values, fine_diagonal = single_step(values_ext, 0)
+
+    def fine_solve(values, low, high):
+        row_rel = face_terms(reluct[low:high], 0)
+        row_sat = face_terms(satur[low:high], 0)
+        col_rel = face_terms(reluct[low:high], 1)
+        col_sat = face_terms(satur[low:high], 1)
+        mobile_ext = mobile_all[low:high]
+        src_cos, src_sin = cos_all[low:high], sin_all[low:high]
+
+        def single_step(values, step_index):
+            divergence, diagonal = flux_terms(values, row_rel, row_sat, col_rel, col_sat)
+            phase_angle = (slice_index * FINE + step_index).astype(jnp.float32) * scale
+            current = src_cos * jnp.cos(phase_angle) + src_sin * jnp.sin(phase_angle)
+            return values + mobile_ext * (divergence + current), diagonal
+
+        fine_values, fine_diagonal = single_step(values, 0)
         for step_index in range(1, FINE):
             fine_values = single_step(fine_values, step_index)[0]
-        fine_end = fine_values[width : width + rows]
-        diagonal = fine_diagonal[width : width + rows]
+        return fine_values, fine_diagonal
+
+    values_ext = extended[0]
+    low, high = 0, rows + 2 * reach
+    for sweep in range(ITERS):
+        last = sweep == ITERS - 1
+        if low == high:
+            values_ext = with_halo(field_now, width)
+            low, high = reach - width, reach + rows + width
+        fine_values, fine_diagonal = fine_solve(values_ext, low, high)
+        keep_low, keep_high = FINE, high - low - FINE
+        fine_end = fine_values[keep_low:keep_high]
+        diagonal = fine_diagonal[keep_low:keep_high]
+        start_now = values_ext[keep_low:keep_high]
+        mobile = mobile_all[low + keep_low : low + keep_high]
         decay = 1.0 / (1.0 + FINE * mobile * diagonal)
         decay = jnp.where(keep_map, decay, 0.0)
-        offset = fine_end - decay * field_now
-        last = sweep == ITERS - 1
+        offset = fine_end - decay * start_now
         field_now, jumps = transposed_states(decay, offset, [fine_end] if last else [])
+        values_ext = field_now
+        low, high = low + keep_low, low + keep_high
+        if high - low == rows:
+            low = high
     return (field_now[None], jumps)
 
 

time: 135 us -> 130 us (0.963)
  blocking collectives: 97.4 us -> 42.2 us
  waiting for transfers between devices: 4.64 us -> 37.1 us
  starting transfers between devices: 13.5 us -> 29.8 us
  other arithmetic: 11.6 us -> 13.4 us
    all_to_all x2 -> x1, blocking collectives: 59.2 us -> 22.5 us  [transposed_states(): cells = lax.all_to_all(parts, 'tm', 1, 1, tiled=True)]
    all_to_all x0 -> x2, waiting for transfers between devices: none -> 34.7 us  [the longest x1 18.6 us: transposed_states(): cells = lax.all_to_all(parts, 'tm', 1, 1, tiled=True)]
    all_to_all x0 -> x2, starting transfers between devices: none -> 24.5 us  [the longest x1 20.1 us: transposed_states(): cells = lax.all_to_all(parts, 'tm', 1, 1, tiled=True)]
    all_to_all x2 -> x1, blocking collectives: 38.2 us -> 19.7 us  [transposed_states(): back = lax.all_to_all(jnp.stack(outs), 'tm', 1, 1, tiled=True)]
    ppermute x2 -> x1, starting transfers between devices: 9.11 us -> 3.12 us  [with_halo(): lax.ppermute(lax.slice_in_dim(block, rows - width, rows, axis=block.ndim...]
    ppermute x2 -> x1, starting transfers between devices: 4.38 us -> 2.16 us  [with_halo(): lax.ppermute(lax.slice_in_dim(block, 0, width, axis=block.ndim - 2), 'spa...]
    ppermute x2 -> x1, waiting for transfers between devices: 4.63 us -> 2.48 us  [with_halo(): lax.ppermute(lax.slice_in_dim(block, 0, width, axis=block.ndim - 2), 'spa...]
  transfers between devices with their start and end apart: 4 -> 4, of which waited for: 1 -> 3; matrix products, arithmetic and copies ran while one was open for 1% -> 0% of each run, Pallas kernels for 0% -> 0%
where the time goes in v3:
time: 130 us
  blocking collectives  42.2 us (32%)
  waiting for transfers between devices  37.1 us (29%)
  starting transfers between devices  29.8 us (23%)
  other arithmetic  13.4 us (10%)
  between operations  4.81 us (4%)
  local copies, waits for them, and re-layouts  2.17 us (2%)
    all_to_all x1, blocking collectives, transposed_states(): cells = lax.all_to_all(parts, 'tm', 1, 1, tiled=True)  22.5 us
    all_to_all x1, starting transfers between devices, transposed_states(): cells = lax.all_to_all(parts, 'tm', 1, 1, tiled=True)  20.1 us
    all_to_all x1, blocking collectives, transposed_states(): back = lax.all_to_all(jnp.stack(outs), 'tm', 1, 1, tiled=True)  19.7 us
    all_to_all x1, waiting for transfers between devices, transposed_states(): cells = lax.all_to_all(parts, 'tm', 1, 1, tiled=True)  18.6 us
    all_to_all x1, waiting for transfers between devices, transposed_states(): back = lax.all_to_all(jnp.stack(outs), 'tm', 1, 1, tiled=True)  16.1 us
    all_to_all x1, starting transfers between devices, transposed_states(): back = lax.all_to_all(jnp.stack(outs), 'tm', 1, 1, tiled=True)  4.43 us
    mul x32, other arithmetic, flux_terms(): col_flux = col_w * col_diff  3.87 us
    ppermute x1, starting transfers between devices, with_halo(): lax.ppermute(lax.slice_in_dim(block, rows - width, rows, axis=block.ndim...  3.12 us
  transfers between devices with their start and end apart: 4, of which 3 were waited for; matrix products, arithmetic and copies ran while one was open for 0% of the time, Pallas kernels for 0%

profile of v3, /device:TPU:7, one launch (start us, length us, event | category | flops | bytes accessed | tf_op | source)
XLA Modules:
  0.0 129.6 jit_solution(11433441609002414081)
XLA Ops:
  0.6 0.8 add_bitcast_fusion.2
  1.5 0.8 pad_maximum_fusion.1
  2.2 3.1 %collective-permute-start = (f32[4,32,256]{2,1,0:T(8,128)S(1)}, f32[4,32,256]{2,1,0:T(8,128)S(1)}, u32[]{:S(2)}, u32[]{:S(2)}) collective-permute-start(f32[4,32,256]{2,1,0:T(8,128)S(1)} %pad_maximum_fusion.1), channel_id=1, source_target_pairs={{0,1},{1,2},{2,3},{3,4},{4,5},{5,6},{6,7},{8,9},{9,10},{10,11},{11... | collective-permute-start | bytes 393224 | tf_op jit(solution)/shard_map/ppermute | solution.py:23
  5.4 2.2 %collective-permute-start.1 = (f32[4,32,256]{2,1,0:T(8,128)S(1)}, f32[4,32,256]{2,1,0:T(8,128)S(1)}, u32[]{:S(2)}, u32[]{:S(2)}) collective-permute-start(f32[4,32,256]{2,1,0:T(8,128)S(1)} %pad_maximum_fusion.1), channel_id=1, source_target_pairs={{1,0},{2,1},{3,2},{4,3},{5,4},{6,5},{7,6},{9,8},{10,9},{11,10},{12... | collective-permute-start | bytes 393224 | tf_op jit(solution)/shard_map/ppermute | solution.py:24
  10.7 2.5 %collective-permute-done.1 = f32[4,32,256]{2,1,0:T(8,128)S(1)} collective-permute-done((f32[4,32,256]{2,1,0:T(8,128)S(1)}, f32[4,32,256]{2,1,0:T(8,128)S(1)}, u32[]{:S(2)}, u32[]{:S(2)}) %collective-permute-start.1) | collective-permute-done | bytes 131104 | tf_op jit(solution)/shard_map/ppermute | solution.py:24
  13.5 0.2 fusion.175
  13.7 0.1 fusion.188
  13.9 0.1 multiply_multiply_fusion.14
  14.2 0.1 multiply_multiply_fusion.13
  14.5 0.1 multiply_multiply_fusion.12
  14.8 0.1 multiply_multiply_fusion.11
  15.1 0.1 multiply_multiply_fusion.10
  15.4 0.1 multiply_multiply_fusion.9
  15.7 0.1 multiply_multiply_fusion.8
  16.0 0.1 multiply_multiply_fusion.7
  16.3 0.1 multiply_multiply_fusion.6
  16.6 0.1 multiply_multiply_fusion.5
  16.9 0.1 multiply_multiply_fusion.4
  17.2 0.1 multiply_multiply_fusion.3
  17.5 0.1 multiply_multiply_fusion.2
  17.8 0.1 multiply_multiply_fusion.1
  18.1 0.1 multiply_multiply_fusion
  18.5 0.8 pad_maximum_fusion.2
  19.3 20.1 %all-to-all-start = ((f32[2,64,256]{2,0,1:T(2,128)}), f32[2,64,256]{2,0,1:T(2,128)S(1)}, u32[]{:S(2)}, u32[]{:S(2)}) async-start(f32[2,64,256]{2,0,1:T(2,128)} %pad_maximum_fusion.2), calls=%async_computation | async-start | bytes 262144 | tf_op jit(solution)/shard_map/all_to_all | solution.py:98
  39.4 18.6 %all-to-all-done = f32[2,64,256]{2,0,1:T(2,128)S(1)} async-done(((f32[2,64,256]{2,0,1:T(2,128)}), f32[2,64,256]{2,0,1:T(2,128)S(1)}, u32[]{:S(2)}, u32[]{:S(2)}) %all-to-all-start) | async-done | bytes 131104 | tf_op jit(solution)/shard_map/all_to_all | solution.py:98
  58.2 0.2 multiply_add_fusion.4
  58.4 0.2 multiply_add_fusion.3
  58.6 0.2 multiply_add_fusion.2
  58.8 0.2 multiply_add_fusion.1
  59.0 0.1 multiply_add_fusion
  59.3 0.7 pad_add_fusion
  60.0 4.4 %all-to-all-start.1 = ((f32[1,64,256]{2,0,1:T(1,128)}), f32[1,64,256]{2,0,1:T(1,128)S(1)}, u32[]{:S(2)}, u32[]{:S(2)}) async-start(f32[1,64,256]{2,0,1:T(1,128)} %pad_add_fusion), calls=%async_computation.1 | async-start | bytes 131072 | tf_op jit(solution)/shard_map/all_to_all | solution.py:114
  64.5 16.1 %all-to-all-done.1 = f32[1,64,256]{2,0,1:T(1,128)S(1)} async-done(((f32[1,64,256]{2,0,1:T(1,128)}), f32[1,64,256]{2,0,1:T(1,128)S(1)}, u32[]{:S(2)}, u32[]{:S(2)}) %all-to-all-start.1) | async-done | bytes 65568 | tf_op jit(solution)/shard_map/all_to_all | solution.py:114
  80.6 0.2 fusion.177
  80.9 0.1 multiply_multiply_fusion.44
  81.2 0.1 multiply_multiply_fusion.43
  81.4 0.1 multiply_multiply_fusion.42
  81.7 0.1 multiply_multiply_fusion.41
  81.9 0.1 multiply_multiply_fusion.40
  82.2 0.1 multiply_multiply_fusion.39
  83.0 0.1 multiply_multiply_fusion.36
  83.2 0.1 multiply_multiply_fusion.35
  83.5 0.1 multiply_multiply_fusion.34
  85.0 22.5 %all_to_all.20 = f32[3,64,128]{2,0,1:T(4,128)S(1)} all-to-all(f32[3,64,128]{2,0,1:T(4,128)S(1)} %pad_maximum_fusion.3), channel_id=1, replica_groups=mesh['tm'=64,'space'=8] {'tm'}, dimensions={1} | all-to-all | bytes 196608 | tf_op jit(solution)/shard_map/all_to_all | solution.py:98
  108.4 19.7 %all_to_all.21 = f32[2,64,128]{2,0,1:T(2,128)S(1)} all-to-all(f32[2,64,128]{2,0,1:T(2,128)S(1)} %pad_maximum_fusion.4), channel_id=1, replica_groups=mesh['tm'=64,'space'=8] {'tm'}, dimensions={1} | all-to-all | bytes 131072 | tf_op jit(solution)/shard_map/all_to_all | solution.py:114
  128.2 0.2 slice_reduce_fusion
  128.3 0.6 slice.1373
  128.9 0.6 slice.1375
  (133 shorter events, 7.0 us)
Async XLA Ops:
  0.6 0.8 copy-start
  2.2 8.5 %collective-permute-start = (f32[4,32,256]{2,1,0:T(8,128)S(1)}, f32[4,32,256]{2,1,0:T(8,128)S(1)}, u32[]{:S(2)}, u32[]{:S(2)}) collective-permute-start(f32[4,32,256]{2,1,0:T(8,128)S(1)} %pad_maximum_fusion.1), channel_id=1, source_target_pairs={{0,1},{1,2},{2,3},{3,4},{4,5},{5,6},{6,7},{8,9},{9,10},{10,11},{11... | collective-permute-start | bytes 393224 | tf_op jit(solution)/shard_map/ppermute | solution.py:23
  5.4 7.8 %collective-permute-start.1 = (f32[4,32,256]{2,1,0:T(8,128)S(1)}, f32[4,32,256]{2,1,0:T(8,128)S(1)}, u32[]{:S(2)}, u32[]{:S(2)}) collective-permute-start(f32[4,32,256]{2,1,0:T(8,128)S(1)} %pad_maximum_fusion.1), channel_id=1, source_target_pairs={{1,0},{2,1},{3,2},{4,3},{5,4},{6,5},{7,6},{9,8},{10,9},{11,10},{12... | collective-permute-start | bytes 393224 | tf_op jit(solution)/shard_map/ppermute | solution.py:24
  9.4 3.8 %copy-start.1 = (f32[1,32,256]{2,1,0:T(8,128)S(1)}, f32[1,32,256]{2,1,0:T(8,128)}, u32[]{:S(2)}) copy-start(f32[1,32,256]{2,1,0:T(8,128)} %param.4) | copy-start | bytes 98308
  19.3 38.7 %all-to-all-start = ((f32[2,64,256]{2,0,1:T(2,128)}), f32[2,64,256]{2,0,1:T(2,128)S(1)}, u32[]{:S(2)}, u32[]{:S(2)}) async-start(f32[2,64,256]{2,0,1:T(2,128)} %pad_maximum_fusion.2), calls=%async_computation | async-start | bytes 262144 | tf_op jit(solution)/shard_map/all_to_all | solution.py:98
  60.0 20.5 %all-to-all-start.1 = ((f32[1,64,256]{2,0,1:T(1,128)}), f32[1,64,256]{2,0,1:T(1,128)S(1)}, u32[]{:S(2)}, u32[]{:S(2)}) async-start(f32[1,64,256]{2,0,1:T(1,128)} %pad_add_fusion), calls=%async_computation.1 | async-start | bytes 131072 | tf_op jit(solution)/shard_map/all_to_all | solution.py:114

commit v4 on v3

--- a/solution.py
+++ b/solution.py
@@ -116,12 +116,31 @@
     return back[0], (back[1:] if extra else None)
 
 
+def scan_over_time(factor, shift):
+    count = factor.shape[0]
+    span = 1
+    while span < count:
+        earlier_factor = shift_down(factor[None], span, 1.0)[0]
+        earlier_shift = shift_down(shift[None], span, 0.0)[0]
+        factor, shift = factor * earlier_factor, factor * earlier_shift + shift
+        span *= 2
+    closing = shift[count - 1 :]
+    before_factor = shift_down(factor[None], 1, 1.0)[0]
+    before_shift = shift_down(shift[None], 1, 0.0)[0]
+    return before_factor * closing + before_shift
+
+
+def exchange(parts):
+    return lax.all_to_all(parts, "tm", 1, 1, tiled=True)
+
+
 def on_device(start_states, region_map, source, front):
     field_now = start_states[0]
     rows, cols = field_now.shape
     width = FINE
-    reach = ITERS * FINE if ITERS * FINE <= rows else FINE
     slices = lax.axis_size("tm")
+    reach = 2 * FINE
+    assert ITERS == 2 and reach <= rows and (rows * cols) % slices == 0 and (2 * width * cols) % slices == 0
     slice_index = lax.axis_index("tm")
     scale = 2.0 * math.pi / (slices * FINE)
 
@@ -154,30 +173,39 @@
         fine_values, fine_diagonal = single_step(values, 0)
         for step_index in range(1, FINE):
             fine_values = single_step(fine_values, step_index)[0]
-        return fine_values, fine_diagonal
-
-    values_ext = extended[0]
-    low, high = 0, rows + 2 * reach
-    for sweep in range(ITERS):
-        last = sweep == ITERS - 1
-        if low == high:
-            values_ext = with_halo(field_now, width)
-            low, high = reach - width, reach + rows + width
-        fine_values, fine_diagonal = fine_solve(values_ext, low, high)
-        keep_low, keep_high = FINE, high - low - FINE
-        fine_end = fine_values[keep_low:keep_high]
-        diagonal = fine_diagonal[keep_low:keep_high]
-        start_now = values_ext[keep_low:keep_high]
-        mobile = mobile_all[low + keep_low : low + keep_high]
-        decay = 1.0 / (1.0 + FINE * mobile * diagonal)
-        decay = jnp.where(keep_map, decay, 0.0)
-        offset = fine_end - decay * start_now
-        field_now, jumps = transposed_states(decay, offset, [fine_end] if last else [])
-        values_ext = field_now
-        low, high = low + keep_low, low + keep_high
-        if high - low == rows:
-            low = high
-    return (field_now[None], jumps)
+        fine_values = fine_values[FINE : high - low - FINE]
+        fine_diagonal = fine_diagonal[FINE : high - low - FINE]
+        mobile = mobile_all[low + FINE : high - FINE]
+        decay = 1.0 / (1.0 + FINE * mobile * fine_diagonal)
+        return fine_values, jnp.where(keep_map, decay, 0.0)
+
+    own_cells = rows * cols // slices
+
+    def to_chunks(block):
+        own = block[width : width + rows].reshape(slices, own_cells)
+        halo = jnp.concatenate([block[:width], block[width + rows :]], 0).reshape(slices, -1)
+        return jnp.concatenate([own, halo], 1)
+
+    def from_chunks(chunks):
+        own = chunks[:, :own_cells].reshape(rows, cols)
+        halo = chunks[:, own_cells:].reshape(2 * width, cols)
+        return jnp.concatenate([halo[:width], own, halo[width:]], 0)
+
+    fine_end, decay = fine_solve(extended[0], 0, rows + 2 * reach)
+    offset = fine_end - decay * extended[0][width : width + rows + 2 * width]
+    timed = exchange(jnp.stack([to_chunks(decay), to_chunks(offset)]))
+    states_timed = scan_over_time(timed[0], timed[1])
+    strip_timed = states_timed[:, :own_cells]
+    field_block = from_chunks(exchange(states_timed[None])[0])
+
+    fine_end, decay = fine_solve(field_block, width, rows + 3 * width)
+    timed = exchange(jnp.stack([decay.reshape(slices, own_cells), fine_end.reshape(slices, own_cells)]))
+    offset_timed = timed[1] - timed[0] * strip_timed
+    states_timed = scan_over_time(timed[0], offset_timed)
+    ends_timed = timed[1]
+    jumps_timed = jnp.concatenate([ends_timed[slices - 1 :], ends_timed[: slices - 1]], 0) - states_timed
+    back = exchange(jnp.stack([states_timed, jumps_timed])).reshape(2, 1, rows, cols)
+    return (back[0], back[1])
 
 
 def solution(mesh):

time: 130 us -> 127 us (0.977)
  blocking collectives: 42.2 us -> 58.2 us
  starting transfers between devices: 29.8 us -> 14.1 us
  waiting for transfers between devices: 37.1 us -> 34.9 us
  other arithmetic: 13.4 us -> 11.5 us
    all_to_all x2, blocking collectives: 42.2 us -> 58.2 us  [exchange(): return lax.all_to_all(parts, 'tm', 1, 1, tiled=True)]
    all_to_all x2, starting transfers between devices: 24.5 us -> 8.85 us  [exchange(): return lax.all_to_all(parts, 'tm', 1, 1, tiled=True)]
    all_to_all x2, waiting for transfers between devices: 34.7 us -> 32.5 us  [exchange(): return lax.all_to_all(parts, 'tm', 1, 1, tiled=True)]
    add x15 -> x9, other arithmetic: 2.16 us -> 0.18 us  [scan_over_time(): factor, shift = (factor * earlier_factor, factor * earlier_shift + shift)]
    add x29 -> x30, other arithmetic: 2.91 us -> 2.94 us  [single_step(): return (values + mobile_ext * (divergence + current), diagonal)]
where the time goes in v4:
time: 127 us
  blocking collectives  58.2 us (46%)
  waiting for transfers between devices  34.9 us (27%)
  starting transfers between devices  14.1 us (11%)
  other arithmetic  11.5 us (9%)
  between operations  4.98 us (4%)
  local copies, waits for them, and re-layouts  3.14 us (2%)
    all_to_all x2, blocking collectives, exchange(): return lax.all_to_all(parts, 'tm', 1, 1, tiled=True)  58.2 us
    all_to_all x2, waiting for transfers between devices, exchange(): return lax.all_to_all(parts, 'tm', 1, 1, tiled=True)  32.5 us
    all_to_all x2, starting transfers between devices, exchange(): return lax.all_to_all(parts, 'tm', 1, 1, tiled=True)  8.85 us
    mul x32, other arithmetic, flux_terms(): col_flux = col_w * col_diff  3.87 us
    ppermute x1, starting transfers between devices, with_halo(): lax.ppermute(lax.slice_in_dim(block, rows - width, rows, axis=block.ndim...  3.12 us
    add x30, other arithmetic, single_step(): return (values + mobile_ext * (divergence + current), diagonal)  2.94 us
  transfers between devices with their start and end apart: 4, of which 3 were waited for; matrix products, arithmetic and copies ran while one was open for 0% of the time, Pallas kernels for 0%

profile of v4, /device:TPU:7, one launch (start us, length us, event | category | flops | bytes accessed | tf_op | source)
XLA Modules:
  0.0 126.9 jit_solution(16339329607477478677)
XLA Ops:
  0.6 0.8 add_bitcast_fusion.2
  1.5 0.8 pad_maximum_fusion.1
  2.2 3.1 %collective-permute-start = (f32[4,32,256]{2,1,0:T(8,128)S(1)}, f32[4,32,256]{2,1,0:T(8,128)S(1)}, u32[]{:S(2)}, u32[]{:S(2)}) collective-permute-start(f32[4,32,256]{2,1,0:T(8,128)S(1)} %pad_maximum_fusion.1), channel_id=1, source_target_pairs={{0,1},{1,2},{2,3},{3,4},{4,5},{5,6},{6,7},{8,9},{9,10},{10,11},{11... | collective-permute-start | bytes 393224 | tf_op jit(solution)/shard_map/ppermute | solution.py:23
  5.4 2.2 %collective-permute-start.1 = (f32[4,32,256]{2,1,0:T(8,128)S(1)}, f32[4,32,256]{2,1,0:T(8,128)S(1)}, u32[]{:S(2)}, u32[]{:S(2)}) collective-permute-start(f32[4,32,256]{2,1,0:T(8,128)S(1)} %pad_maximum_fusion.1), channel_id=1, source_target_pairs={{1,0},{2,1},{3,2},{4,3},{5,4},{6,5},{7,6},{9,8},{10,9},{11,10},{12... | collective-permute-start | bytes 393224 | tf_op jit(solution)/shard_map/ppermute | solution.py:24
  10.7 2.5 %collective-permute-done.1 = f32[4,32,256]{2,1,0:T(8,128)S(1)} collective-permute-done((f32[4,32,256]{2,1,0:T(8,128)S(1)}, f32[4,32,256]{2,1,0:T(8,128)S(1)}, u32[]{:S(2)}, u32[]{:S(2)}) %collective-permute-start.1) | collective-permute-done | bytes 131104 | tf_op jit(solution)/shard_map/ppermute | solution.py:24
  13.5 0.2 fusion.184
  13.8 0.1 fusion.199
  13.9 0.1 multiply_multiply_fusion.14
  14.2 0.1 multiply_multiply_fusion.13
  14.5 0.1 multiply_multiply_fusion.12
  14.8 0.1 multiply_multiply_fusion.11
  15.1 0.1 multiply_multiply_fusion.10
  15.4 0.1 multiply_multiply_fusion.9
  15.7 0.1 multiply_multiply_fusion.8
  16.0 0.1 multiply_multiply_fusion.7
  16.3 0.1 multiply_multiply_fusion.6
  16.6 0.1 multiply_multiply_fusion.5
  16.9 0.1 multiply_multiply_fusion.4
  17.2 0.1 multiply_multiply_fusion.3
  17.5 0.1 multiply_multiply_fusion.2
  17.8 0.1 multiply_multiply_fusion.1
  18.1 0.1 multiply_multiply_fusion
  18.7 0.1 pad_maximum_fusion.2
  18.8 38.5 %all_to_all.20 = f32[2,64,256]{2,0,1:T(2,128)S(1)} all-to-all(f32[2,64,256]{2,0,1:T(2,128)S(1)} %pad_maximum_fusion.2), channel_id=1, replica_groups=mesh['tm'=64,'space'=8] {'tm'}, dimensions={1} | all-to-all | bytes 262144 | tf_op jit(solution)/shard_map/all_to_all | solution.py:134
  57.9 0.7 copy.32
  58.6 4.4 %all-to-all-start.1 = ((f32[1,64,256]{2,0,1:T(1,128)}), f32[1,64,256]{2,0,1:T(1,128)S(1)}, u32[]{:S(2)}, u32[]{:S(2)}) async-start(f32[1,64,256]{2,0,1:T(1,128)} %copy.32), calls=%async_computation.1 | async-start | bytes 131072 | tf_op jit(solution)/shard_map/all_to_all | solution.py:134
  63.0 16.2 %all-to-all-done.1 = f32[1,64,256]{2,0,1:T(1,128)S(1)} async-done(((f32[1,64,256]{2,0,1:T(1,128)}), f32[1,64,256]{2,0,1:T(1,128)S(1)}, u32[]{:S(2)}, u32[]{:S(2)}) %all-to-all-start.1) | async-done | bytes 65568 | tf_op jit(solution)/shard_map/all_to_all | solution.py:134
  79.4 0.2 fusion.186
  79.7 0.1 multiply_multiply_fusion.44
  80.0 0.1 multiply_multiply_fusion.43
  80.3 0.1 multiply_multiply_fusion.42
  80.5 0.1 multiply_multiply_fusion.41
  80.8 0.1 multiply_multiply_fusion.40
  81.0 0.1 multiply_multiply_fusion.39
  81.3 0.1 multiply_multiply_fusion.38
  81.5 0.1 multiply_multiply_fusion.37
  81.8 0.1 multiply_multiply_fusion.36
  82.1 0.1 multiply_multiply_fusion.35
  82.3 0.1 multiply_multiply_fusion.34
  82.6 0.1 multiply_multiply_fusion.33
  82.8 0.1 multiply_multiply_fusion.32
  83.8 0.7 pad_maximum_fusion.5
  84.5 4.4 %all-to-all-start.2 = ((f32[2,64,128]{2,0,1:T(2,128)}), f32[2,64,128]{2,0,1:T(2,128)S(1)}, u32[]{:S(2)}, u32[]{:S(2)}) async-start(f32[2,64,128]{2,0,1:T(2,128)} %pad_maximum_fusion.5), calls=%async_computation.2 | async-start | bytes 131072 | tf_op jit(solution)/shard_map/all_to_all | solution.py:134
  88.9 16.3 %all-to-all-done.2 = f32[2,64,128]{2,0,1:T(2,128)S(1)} async-done(((f32[2,64,128]{2,0,1:T(2,128)}), f32[2,64,128]{2,0,1:T(2,128)S(1)}, u32[]{:S(2)}, u32[]{:S(2)}) %all-to-all-start.2) | async-done | bytes 65568 | tf_op jit(solution)/shard_map/all_to_all | solution.py:134
  105.8 19.7 %all_to_all.21 = f32[2,64,128]{2,0,1:T(2,128)S(1)} all-to-all(f32[2,64,128]{2,0,1:T(2,128)S(1)} %copy.38), channel_id=1, replica_groups=mesh['tm'=64,'space'=8] {'tm'}, dimensions={1} | all-to-all | bytes 131072 | tf_op jit(solution)/shard_map/all_to_all | solution.py:134
  125.5 0.2 slice_reduce_fusion
  125.7 0.6 squeeze.106
  126.3 0.6 squeeze.107
  (157 shorter events, 6.4 us)
Async XLA Ops:
  0.6 0.8 copy-start
  2.2 8.5 %collective-permute-start = (f32[4,32,256]{2,1,0:T(8,128)S(1)}, f32[4,32,256]{2,1,0:T(8,128)S(1)}, u32[]{:S(2)}, u32[]{:S(2)}) collective-permute-start(f32[4,32,256]{2,1,0:T(8,128)S(1)} %pad_maximum_fusion.1), channel_id=1, source_target_pairs={{0,1},{1,2},{2,3},{3,4},{4,5},{5,6},{6,7},{8,9},{9,10},{10,11},{11... | collective-permute-start | bytes 393224 | tf_op jit(solution)/shard_map/ppermute | solution.py:23
  5.4 7.8 %collective-permute-start.1 = (f32[4,32,256]{2,1,0:T(8,128)S(1)}, f32[4,32,256]{2,1,0:T(8,128)S(1)}, u32[]{:S(2)}, u32[]{:S(2)}) collective-permute-start(f32[4,32,256]{2,1,0:T(8,128)S(1)} %pad_maximum_fusion.1), channel_id=1, source_target_pairs={{1,0},{2,1},{3,2},{4,3},{5,4},{6,5},{7,6},{9,8},{10,9},{11,10},{12... | collective-permute-start | bytes 393224 | tf_op jit(solution)/shard_map/ppermute | solution.py:24
  9.4 3.8 %copy-start.1 = (f32[1,32,256]{2,1,0:T(8,128)S(1)}, f32[1,32,256]{2,1,0:T(8,128)}, u32[]{:S(2)}) copy-start(f32[1,32,256]{2,1,0:T(8,128)} %param.4) | copy-start | bytes 98308
  58.6 20.7 %all-to-all-start.1 = ((f32[1,64,256]{2,0,1:T(1,128)}), f32[1,64,256]{2,0,1:T(1,128)S(1)}, u32[]{:S(2)}, u32[]{:S(2)}) async-start(f32[1,64,256]{2,0,1:T(1,128)} %copy.32), calls=%async_computation.1 | async-start | bytes 131072 | tf_op jit(solution)/shard_map/all_to_all | solution.py:134
  84.5 20.7 %all-to-all-start.2 = ((f32[2,64,128]{2,0,1:T(2,128)}), f32[2,64,128]{2,0,1:T(2,128)S(1)}, u32[]{:S(2)}, u32[]{:S(2)}) async-start(f32[2,64,128]{2,0,1:T(2,128)} %pad_maximum_fusion.5), calls=%async_computation.2 | async-start | bytes 131072 | tf_op jit(solution)/shard_map/all_to_all | solution.py:134

commit v5 on v4

--- a/solution.py
+++ b/solution.py
@@ -156,24 +156,25 @@
     cut_slice = (front - 1) % slices
     keep_map = slice_index != cut_slice
 
-    def fine_solve(values, low, high):
+    def single_step(values, step_index, low, high):
         row_rel = face_terms(reluct[low:high], 0)
         row_sat = face_terms(satur[low:high], 0)
         col_rel = face_terms(reluct[low:high], 1)
         col_sat = face_terms(satur[low:high], 1)
-        mobile_ext = mobile_all[low:high]
-        src_cos, src_sin = cos_all[low:high], sin_all[low:high]
-
-        def single_step(values, step_index):
-            divergence, diagonal = flux_terms(values, row_rel, row_sat, col_rel, col_sat)
-            phase_angle = (slice_index * FINE + step_index).astype(jnp.float32) * scale
-            current = src_cos * jnp.cos(phase_angle) + src_sin * jnp.sin(phase_angle)
-            return values + mobile_ext * (divergence + current), diagonal
-
-        fine_values, fine_diagonal = single_step(values, 0)
+        divergence, diagonal = flux_terms(values, row_rel, row_sat, col_rel, col_sat)
+        phase_angle = (slice_index * FINE + step_index).astype(jnp.float32) * scale
+        current = cos_all[low:high] * jnp.cos(phase_angle) + sin_all[low:high] * jnp.sin(phase_angle)
+        return values + mobile_all[low:high] * (divergence + current), diagonal
+
+    def fine_solve(values, low, high):
+        fine_values, fine_diagonal = single_step(values, 0, low, high)
+        trim = 0
         for step_index in range(1, FINE):
-            fine_values = single_step(fine_values, step_index)[0]
-        fine_values = fine_values[FINE : high - low - FINE]
+            if step_index >= trim + 8:
+                trim += 8
+                fine_values = fine_values[8:-8]
+            fine_values = single_step(fine_values, step_index, low + trim, high - trim)[0]
+        fine_values = fine_values[FINE - trim : high - low - FINE - trim]
         fine_diagonal = fine_diagonal[FINE : high - low - FINE]
         mobile = mobile_all[low + FINE : high - FINE]
         decay = 1.0 / (1.0 + FINE * mobile * fine_diagonal)
@@ -196,7 +197,7 @@
     timed = exchange(jnp.stack([to_chunks(decay), to_chunks(offset)]))
     states_timed = scan_over_time(timed[0], timed[1])
     strip_timed = states_timed[:, :own_cells]
-    field_block = from_chunks(exchange(states_timed[None])[0])
+    field_block = from_chunks(lax.all_to_all(states_timed, "tm", 0, 0, tiled=True))
 
     fine_end, decay = fine_solve(field_block, width, rows + 3 * width)
     timed = exchange(jnp.stack([decay.reshape(slices, own_cells), fine_end.reshape(slices, own_cells)]))

time: 127 us -> 128 us (level)
  blocking collectives: 58.2 us -> 19.7 us
  starting transfers between devices: 14.1 us -> 34.2 us
  waiting for transfers between devices: 34.9 us -> 53.2 us
    all_to_all x2 -> x1, blocking collectives: 58.2 us -> 19.7 us  [exchange(): return lax.all_to_all(parts, 'tm', 1, 1, tiled=True)]
    all_to_all x0 -> x1, waiting for transfers between devices: none -> 16.1 us  [on_device(): lax.all_to_all(states_timed, 'tm', 0, 0, tiled=True)]
    all_to_all x2, starting transfers between devices: 8.85 us -> 24.5 us  [exchange(): return lax.all_to_all(parts, 'tm', 1, 1, tiled=True)]
    all_to_all x0 -> x1, starting transfers between devices: none -> 4.42 us  [on_device(): lax.all_to_all(states_timed, 'tm', 0, 0, tiled=True)]
    all_to_all x2, waiting for transfers between devices: 32.5 us -> 34.6 us  [exchange(): return lax.all_to_all(parts, 'tm', 1, 1, tiled=True)]
    add x30 -> x31, other arithmetic: 2.94 us -> 2.72 us  [the longest x30 2.7 us: single_step(): return (values + mobile_all[low:high] * (divergence + current), diagonal)]
  transfers between devices with their start and end apart: 4 -> 5, of which waited for: 3 -> 4; matrix products, arithmetic and copies ran while one was open for 0% -> 0% of each run, Pallas kernels for 0% -> 0%
where the time goes in v5:
time: 128 us; the launch traced here: 127 us
  waiting for transfers between devices  53.2 us (42%)
  starting transfers between devices  34.2 us (27%)
  blocking collectives  19.7 us (15%)
  other arithmetic  11.9 us (9%)
  between operations  5.08 us (4%)
  local copies, waits for them, and re-layouts  3.32 us (3%)
    all_to_all x2, waiting for transfers between devices, exchange(): return lax.all_to_all(parts, 'tm', 1, 1, tiled=True)  34.6 us
    all_to_all x2, starting transfers between devices, exchange(): return lax.all_to_all(parts, 'tm', 1, 1, tiled=True)  24.5 us
    all_to_all x1, blocking collectives, exchange(): return lax.all_to_all(parts, 'tm', 1, 1, tiled=True)  19.7 us
    all_to_all x1, waiting for transfers between devices, on_device(): lax.all_to_all(states_timed, 'tm', 0, 0, tiled=True)  16.1 us
    all_to_all x1, starting transfers between devices, on_device(): lax.all_to_all(states_timed, 'tm', 0, 0, tiled=True)  4.42 us
    mul x32, other arithmetic, flux_terms(): col_flux = col_w * col_diff  3.83 us
    ppermute x1, starting transfers between devices, with_halo(): lax.ppermute(lax.slice_in_dim(block, rows - width, rows, axis=block.ndim...  3.12 us
    add x30, other arithmetic, single_step(): return (values + mobile_all[low:high] * (divergence + current), diagonal)  2.7 us
  transfers between devices with their start and end apart: 5, of which 4 were waited for; matrix products, arithmetic and copies ran while one was open for 0% of the time, Pallas kernels for 0%

profile of v5, /device:TPU:7, one launch (start us, length us, event | category | flops | bytes accessed | tf_op | source)
XLA Modules:
  0.0 127.4 jit_solution(519434310999160702)
XLA Ops:
  0.6 0.8 add_bitcast_fusion.4
  1.5 0.8 pad_maximum_fusion.1
  2.2 3.1 %collective-permute-start = (f32[4,32,256]{2,1,0:T(8,128)S(1)}, f32[4,32,256]{2,1,0:T(8,128)S(1)}, u32[]{:S(2)}, u32[]{:S(2)}) collective-permute-start(f32[4,32,256]{2,1,0:T(8,128)S(1)} %pad_maximum_fusion.1), channel_id=1, source_target_pairs={{0,1},{1,2},{2,3},{3,4},{4,5},{5,6},{6,7},{8,9},{9,10},{10,11},{11... | collective-permute-start | bytes 393224 | tf_op jit(solution)/shard_map/ppermute | solution.py:23
  5.4 2.2 %collective-permute-start.1 = (f32[4,32,256]{2,1,0:T(8,128)S(1)}, f32[4,32,256]{2,1,0:T(8,128)S(1)}, u32[]{:S(2)}, u32[]{:S(2)}) collective-permute-start(f32[4,32,256]{2,1,0:T(8,128)S(1)} %pad_maximum_fusion.1), channel_id=1, source_target_pairs={{1,0},{2,1},{3,2},{4,3},{5,4},{6,5},{7,6},{9,8},{10,9},{11,10},{12... | collective-permute-start | bytes 393224 | tf_op jit(solution)/shard_map/ppermute | solution.py:24
  10.7 2.5 %collective-permute-done.1 = f32[4,32,256]{2,1,0:T(8,128)S(1)} collective-permute-done((f32[4,32,256]{2,1,0:T(8,128)S(1)}, f32[4,32,256]{2,1,0:T(8,128)S(1)}, u32[]{:S(2)}, u32[]{:S(2)}) %collective-permute-start.1) | collective-permute-done | bytes 131104 | tf_op jit(solution)/shard_map/ppermute | solution.py:24
  13.5 0.2 fusion.198
  13.8 0.1 fusion.219
  13.9 0.1 multiply_multiply_fusion.6
  14.1 0.1 fusion.58
  14.2 0.1 multiply_multiply_fusion.5
  14.4 0.1 fusion.54
  14.5 0.1 multiply_multiply_fusion.4
  14.7 0.1 fusion.50
  14.8 0.1 multiply_multiply_fusion.3
  15.1 0.1 multiply_multiply_fusion.2
  15.4 0.1 multiply_multiply_fusion.1
  15.6 0.1 fusion.38
  15.7 0.1 multiply_multiply_fusion
  16.1 0.2 multiply_multiply_fusion.14
  16.4 0.1 multiply_multiply_fusion.13
  16.7 0.1 multiply_multiply_fusion.12
  17.0 0.1 multiply_multiply_fusion.11
  17.3 0.1 multiply_multiply_fusion.10
  17.5 0.1 multiply_multiply_fusion.9
  17.8 0.1 multiply_multiply_fusion.8
  18.1 0.1 multiply_multiply_fusion.7
  18.7 0.8 pad_maximum_fusion.2
  19.5 20.1 %all-to-all-start = ((f32[2,64,256]{2,0,1:T(2,128)}), f32[2,64,256]{2,0,1:T(2,128)S(1)}, u32[]{:S(2)}, u32[]{:S(2)}) async-start(f32[2,64,256]{2,0,1:T(2,128)} %pad_maximum_fusion.2), calls=%async_computation | async-start | bytes 262144 | tf_op jit(solution)/shard_map/all_to_all | solution.py:134
  39.6 18.6 %all-to-all-done = f32[2,64,256]{2,0,1:T(2,128)S(1)} async-done(((f32[2,64,256]{2,0,1:T(2,128)}), f32[2,64,256]{2,0,1:T(2,128)S(1)}, u32[]{:S(2)}, u32[]{:S(2)}) %all-to-all-start) | async-done | bytes 131104 | tf_op jit(solution)/shard_map/all_to_all | solution.py:134
  58.7 0.7 copy.31
  59.4 4.4 %all-to-all-start.1 = ((f32[64,1,256]{2,1,0:T(1,128)}), f32[64,1,256]{2,1,0:T(1,128)S(1)}, u32[]{:S(2)}, u32[]{:S(2)}) async-start(f32[64,1,256]{2,1,0:T(1,128)} %copy.31), calls=%async_computation.1 | async-start | bytes 131072 | tf_op jit(solution)/shard_map/all_to_all | solution.py:200
  63.9 16.1 %all-to-all-done.1 = f32[64,1,256]{2,1,0:T(1,128)S(1)} async-done(((f32[64,1,256]{2,1,0:T(1,128)}), f32[64,1,256]{2,1,0:T(1,128)S(1)}, u32[]{:S(2)}, u32[]{:S(2)}) %all-to-all-start.1) | async-done | bytes 65568 | tf_op jit(solution)/shard_map/all_to_all | solution.py:200
  80.1 0.2 fusion.200
  80.4 0.1 multiply_multiply_fusion.28
  80.7 0.1 multiply_multiply_fusion.27
  81.0 0.1 multiply_multiply_fusion.26
  81.2 0.1 multiply_multiply_fusion.25
  81.5 0.1 multiply_multiply_fusion.24
  81.7 0.1 multiply_multiply_fusion.23
  82.0 0.1 multiply_multiply_fusion.22
  82.3 0.1 multiply_multiply_fusion.44
  84.4 0.7 pad_maximum_fusion.5
  85.1 4.4 %all-to-all-start.2 = ((f32[2,64,128]{2,0,1:T(2,128)}), f32[2,64,128]{2,0,1:T(2,128)S(1)}, u32[]{:S(2)}, u32[]{:S(2)}) async-start(f32[2,64,128]{2,0,1:T(2,128)} %pad_maximum_fusion.5), calls=%async_computation.2 | async-start | bytes 131072 | tf_op jit(solution)/shard_map/all_to_all | solution.py:134
  89.6 16.1 %all-to-all-done.2 = f32[2,64,128]{2,0,1:T(2,128)S(1)} async-done(((f32[2,64,128]{2,0,1:T(2,128)}), f32[2,64,128]{2,0,1:T(2,128)S(1)}, u32[]{:S(2)}, u32[]{:S(2)}) %all-to-all-start.2) | async-done | bytes 65568 | tf_op jit(solution)/shard_map/all_to_all | solution.py:134
  106.2 19.7 %all_to_all.24 = f32[2,64,128]{2,0,1:T(2,128)S(1)} all-to-all(f32[2,64,128]{2,0,1:T(2,128)S(1)} %copy.37), channel_id=1, replica_groups=mesh['tm'=64,'space'=8] {'tm'}, dimensions={1} | all-to-all | bytes 131072 | tf_op jit(solution)/shard_map/all_to_all | solution.py:134
  126.0 0.2 slice_reduce_fusion
  126.1 0.6 squeeze.108
  126.8 0.6 squeeze.109
  (168 shorter events, 6.4 us)
Async XLA Ops:
  0.6 0.8 copy-start
  2.2 8.5 %collective-permute-start = (f32[4,32,256]{2,1,0:T(8,128)S(1)}, f32[4,32,256]{2,1,0:T(8,128)S(1)}, u32[]{:S(2)}, u32[]{:S(2)}) collective-permute-start(f32[4,32,256]{2,1,0:T(8,128)S(1)} %pad_maximum_fusion.1), channel_id=1, source_target_pairs={{0,1},{1,2},{2,3},{3,4},{4,5},{5,6},{6,7},{8,9},{9,10},{10,11},{11... | collective-permute-start | bytes 393224 | tf_op jit(solution)/shard_map/ppermute | solution.py:23
  5.4 7.8 %collective-permute-start.1 = (f32[4,32,256]{2,1,0:T(8,128)S(1)}, f32[4,32,256]{2,1,0:T(8,128)S(1)}, u32[]{:S(2)}, u32[]{:S(2)}) collective-permute-start(f32[4,32,256]{2,1,0:T(8,128)S(1)} %pad_maximum_fusion.1), channel_id=1, source_target_pairs={{1,0},{2,1},{3,2},{4,3},{5,4},{6,5},{7,6},{9,8},{10,9},{11,10},{12... | collective-permute-start | bytes 393224 | tf_op jit(solution)/shard_map/ppermute | solution.py:24
  9.4 3.8 %copy-start.1 = (f32[1,32,256]{2,1,0:T(8,128)S(1)}, f32[1,32,256]{2,1,0:T(8,128)}, u32[]{:S(2)}) copy-start(f32[1,32,256]{2,1,0:T(8,128)} %param.4) | copy-start | bytes 98308
  19.5 38.7 %all-to-all-start = ((f32[2,64,256]{2,0,1:T(2,128)}), f32[2,64,256]{2,0,1:T(2,128)S(1)}, u32[]{:S(2)}, u32[]{:S(2)}) async-start(f32[2,64,256]{2,0,1:T(2,128)} %pad_maximum_fusion.2), calls=%async_computation | async-start | bytes 262144 | tf_op jit(solution)/shard_map/all_to_all | solution.py:134
  59.4 20.5 %all-to-all-start.1 = ((f32[64,1,256]{2,1,0:T(1,128)}), f32[64,1,256]{2,1,0:T(1,128)S(1)}, u32[]{:S(2)}, u32[]{:S(2)}) async-start(f32[64,1,256]{2,1,0:T(1,128)} %copy.31), calls=%async_computation.1 | async-start | bytes 131072 | tf_op jit(solution)/shard_map/all_to_all | solution.py:200
  85.1 20.5 %all-to-all-start.2 = ((f32[2,64,128]{2,0,1:T(2,128)}), f32[2,64,128]{2,0,1:T(2,128)S(1)}, u32[]{:S(2)}, u32[]{:S(2)}) async-start(f32[2,64,128]{2,0,1:T(2,128)} %pad_maximum_fusion.5), calls=%async_computation.2 | async-start | bytes 131072 | tf_op jit(solution)/shard_map/all_to_all | solution.py:134

commit v6 on v4

--- a/solution.py
+++ b/solution.py
@@ -180,15 +180,24 @@
         return fine_values, jnp.where(keep_map, decay, 0.0)
 
     own_cells = rows * cols // slices
+    assert rows % 8 == 0 and cols % 128 == 0 and (2 * width) % 8 == 0
+
+    def cells_of(x):
+        n = x.shape[0]
+        return x.reshape(n // 8, 8, cols // 128, 128).transpose(0, 2, 1, 3).reshape(slices, -1)
+
+    def grid_of(chunks):
+        n = chunks.size // cols
+        return chunks.reshape(n // 8, cols // 128, 8, 128).transpose(0, 2, 1, 3).reshape(n, cols)
 
     def to_chunks(block):
-        own = block[width : width + rows].reshape(slices, own_cells)
-        halo = jnp.concatenate([block[:width], block[width + rows :]], 0).reshape(slices, -1)
+        own = cells_of(block[width : width + rows])
+        halo = cells_of(jnp.concatenate([block[:width], block[width + rows :]], 0))
         return jnp.concatenate([own, halo], 1)
 
     def from_chunks(chunks):
-        own = chunks[:, :own_cells].reshape(rows, cols)
-        halo = chunks[:, own_cells:].reshape(2 * width, cols)
+        own = grid_of(chunks[:, :own_cells])
+        halo = grid_of(chunks[:, own_cells:])
         return jnp.concatenate([halo[:width], own, halo[width:]], 0)
 
     fine_end, decay = fine_solve(extended[0], 0, rows + 2 * reach)
@@ -199,13 +208,13 @@
     field_block = from_chunks(exchange(states_timed[None])[0])
 
     fine_end, decay = fine_solve(field_block, width, rows + 3 * width)
-    timed = exchange(jnp.stack([decay.reshape(slices, own_cells), fine_end.reshape(slices, own_cells)]))
+    timed = exchange(jnp.stack([cells_of(decay), cells_of(fine_end)]))
     offset_timed = timed[1] - timed[0] * strip_timed
     states_timed = scan_over_time(timed[0], offset_timed)
     ends_timed = timed[1]
     jumps_timed = jnp.concatenate([ends_timed[slices - 1 :], ends_timed[: slices - 1]], 0) - states_timed
-    back = exchange(jnp.stack([states_timed, jumps_timed])).reshape(2, 1, rows, cols)
-    return (back[0], back[1])
+    back = exchange(jnp.stack([states_timed, jumps_timed]))
+    return (grid_of(back[0])[None], grid_of(back[1])[None])
 
 
 def solution(mesh):

time: 127 us -> 127 us (level)
  blocking collectives: 58.2 us -> 19.7 us
  starting transfers between devices: 14.1 us -> 34.2 us
  waiting for transfers between devices: 34.9 us -> 53.6 us
    all_to_all x2 -> x1, blocking collectives: 58.2 us -> 19.7 us  [exchange(): return lax.all_to_all(parts, 'tm', 1, 1, tiled=True)]
    all_to_all x2 -> x3, starting transfers between devices: 8.85 us -> 28.9 us  [exchange(): return lax.all_to_all(parts, 'tm', 1, 1, tiled=True)]
    all_to_all x2 -> x3, waiting for transfers between devices: 32.5 us -> 51.1 us  [exchange(): return lax.all_to_all(parts, 'tm', 1, 1, tiled=True)]
  transfers between devices with their start and end apart: 4 -> 5, of which waited for: 3 -> 4; matrix products, arithmetic and copies ran while one was open for 0% -> 0% of each run, Pallas kernels for 0% -> 0%
where the time goes in v6:
time: 127 us
  waiting for transfers between devices  53.6 us (42%)
  starting transfers between devices  34.2 us (27%)
  blocking collectives  19.7 us (16%)
  other arithmetic  12.1 us (10%)
  between operations  4.9 us (4%)
  local copies, waits for them, and re-layouts  2.28 us (2%)
    all_to_all x3, waiting for transfers between devices, exchange(): return lax.all_to_all(parts, 'tm', 1, 1, tiled=True)  51.1 us
    all_to_all x3, starting transfers between devices, exchange(): return lax.all_to_all(parts, 'tm', 1, 1, tiled=True)  28.9 us
    all_to_all x1, blocking collectives, exchange(): return lax.all_to_all(parts, 'tm', 1, 1, tiled=True)  19.7 us
    mul x32, other arithmetic, flux_terms(): col_flux = col_w * col_diff  3.87 us
    ppermute x1, starting transfers between devices, with_halo(): lax.ppermute(lax.slice_in_dim(block, rows - width, rows, axis=block.ndim...  3.12 us
    add x30, other arithmetic, single_step(): return (values + mobile_ext * (divergence + current), diagonal)  2.93 us
  transfers between devices with their start and end apart: 5, of which 4 were waited for; matrix products, arithmetic and copies ran while one was open for 0% of the time, Pallas kernels for 0%

profile of v6, /device:TPU:7, one launch (start us, length us, event | category | flops | bytes accessed | tf_op | source)
XLA Modules:
  0.0 126.7 jit_solution(2999123413913985552)
XLA Ops:
  0.6 0.8 add_bitcast_fusion.2
  1.5 0.8 pad_maximum_fusion.1
  2.2 3.1 %collective-permute-start = (f32[4,32,256]{2,1,0:T(8,128)S(1)}, f32[4,32,256]{2,1,0:T(8,128)S(1)}, u32[]{:S(2)}, u32[]{:S(2)}) collective-permute-start(f32[4,32,256]{2,1,0:T(8,128)S(1)} %pad_maximum_fusion.1), channel_id=1, source_target_pairs={{0,1},{1,2},{2,3},{3,4},{4,5},{5,6},{6,7},{8,9},{9,10},{10,11},{11... | collective-permute-start | bytes 393224 | tf_op jit(solution)/shard_map/ppermute | solution.py:23
  5.4 2.2 %collective-permute-start.1 = (f32[4,32,256]{2,1,0:T(8,128)S(1)}, f32[4,32,256]{2,1,0:T(8,128)S(1)}, u32[]{:S(2)}, u32[]{:S(2)}) collective-permute-start(f32[4,32,256]{2,1,0:T(8,128)S(1)} %pad_maximum_fusion.1), channel_id=1, source_target_pairs={{1,0},{2,1},{3,2},{4,3},{5,4},{6,5},{7,6},{9,8},{10,9},{11,10},{12... | collective-permute-start | bytes 393224 | tf_op jit(solution)/shard_map/ppermute | solution.py:24
  10.7 2.5 %collective-permute-done.1 = f32[4,32,256]{2,1,0:T(8,128)S(1)} collective-permute-done((f32[4,32,256]{2,1,0:T(8,128)S(1)}, f32[4,32,256]{2,1,0:T(8,128)S(1)}, u32[]{:S(2)}, u32[]{:S(2)}) %collective-permute-start.1) | collective-permute-done | bytes 131104 | tf_op jit(solution)/shard_map/ppermute | solution.py:24
  13.5 0.2 fusion.184
  13.7 0.1 fusion.199
  13.9 0.1 multiply_multiply_fusion.14
  14.2 0.1 multiply_multiply_fusion.13
  14.5 0.1 multiply_multiply_fusion.12
  14.8 0.1 multiply_multiply_fusion.11
  15.1 0.1 multiply_multiply_fusion.10
  15.4 0.1 multiply_multiply_fusion.9
  15.7 0.1 multiply_multiply_fusion.8
  16.0 0.1 multiply_multiply_fusion.7
  16.3 0.1 multiply_multiply_fusion.6
  16.6 0.1 multiply_multiply_fusion.5
  16.9 0.1 multiply_multiply_fusion.4
  17.2 0.1 multiply_multiply_fusion.3
  17.5 0.1 multiply_multiply_fusion.2
  17.8 0.1 multiply_multiply_fusion.1
  18.1 0.1 multiply_multiply_fusion
  18.6 0.8 pad_maximum_fusion.2
  19.4 20.1 %all-to-all-start = ((f32[2,64,256]{2,0,1:T(2,128)}), f32[2,64,256]{2,0,1:T(2,128)S(1)}, u32[]{:S(2)}, u32[]{:S(2)}) async-start(f32[2,64,256]{2,0,1:T(2,128)} %pad_maximum_fusion.2), calls=%async_computation | async-start | bytes 262144 | tf_op jit(solution)/shard_map/all_to_all | solution.py:134
  39.5 18.6 %all-to-all-done = f32[2,64,256]{2,0,1:T(2,128)S(1)} async-done(((f32[2,64,256]{2,0,1:T(2,128)}), f32[2,64,256]{2,0,1:T(2,128)S(1)}, u32[]{:S(2)}, u32[]{:S(2)}) %all-to-all-start) | async-done | bytes 131104 | tf_op jit(solution)/shard_map/all_to_all | solution.py:134
  58.6 0.7 copy.32
  59.3 4.4 %all-to-all-start.1 = ((f32[1,64,256]{2,0,1:T(1,128)}), f32[1,64,256]{2,0,1:T(1,128)S(1)}, u32[]{:S(2)}, u32[]{:S(2)}) async-start(f32[1,64,256]{2,0,1:T(1,128)} %copy.32), calls=%async_computation.1 | async-start | bytes 131072 | tf_op jit(solution)/shard_map/all_to_all | solution.py:134
  63.8 16.2 %all-to-all-done.1 = f32[1,64,256]{2,0,1:T(1,128)S(1)} async-done(((f32[1,64,256]{2,0,1:T(1,128)}), f32[1,64,256]{2,0,1:T(1,128)S(1)}, u32[]{:S(2)}, u32[]{:S(2)}) %all-to-all-start.1) | async-done | bytes 65568 | tf_op jit(solution)/shard_map/all_to_all | solution.py:134
  80.1 0.2 fusion.186
  80.4 0.1 multiply_multiply_fusion.44
  80.7 0.1 multiply_multiply_fusion.43
  80.9 0.1 multiply_multiply_fusion.42
  81.2 0.1 multiply_multiply_fusion.41
  81.4 0.1 multiply_multiply_fusion.40
  81.7 0.1 multiply_multiply_fusion.39
  82.0 0.1 multiply_multiply_fusion.38
  82.2 0.1 multiply_multiply_fusion.37
  82.5 0.1 multiply_multiply_fusion.36
  82.7 0.1 multiply_multiply_fusion.35
  83.0 0.1 multiply_multiply_fusion.34
  83.2 0.1 multiply_multiply_fusion.33
  83.5 0.1 multiply_multiply_fusion.32
  83.8 0.1 multiply_multiply_fusion.31
  84.4 0.7 pad_maximum_fusion.6
  85.1 4.4 %all-to-all-start.2 = ((f32[2,64,128]{2,0,1:T(2,128)}), f32[2,64,128]{2,0,1:T(2,128)S(1)}, u32[]{:S(2)}, u32[]{:S(2)}) async-start(f32[2,64,128]{2,0,1:T(2,128)} %pad_maximum_fusion.6), calls=%async_computation.2 | async-start | bytes 131072 | tf_op jit(solution)/shard_map/all_to_all | solution.py:134
  89.5 16.3 %all-to-all-done.2 = f32[2,64,128]{2,0,1:T(2,128)S(1)} async-done(((f32[2,64,128]{2,0,1:T(2,128)}), f32[2,64,128]{2,0,1:T(2,128)S(1)}, u32[]{:S(2)}, u32[]{:S(2)}) %all-to-all-start.2) | async-done | bytes 65568 | tf_op jit(solution)/shard_map/all_to_all | solution.py:134
  106.3 19.7 %all_to_all.20 = f32[2,64,128]{2,0,1:T(2,128)S(1)} all-to-all(f32[2,64,128]{2,0,1:T(2,128)S(1)} %copy.38), channel_id=1, replica_groups=mesh['tm'=64,'space'=8] {'tm'}, dimensions={1} | all-to-all | bytes 131072 | tf_op jit(solution)/shard_map/all_to_all | solution.py:134
  126.1 0.7 fusion.207
  (145 shorter events, 6.1 us)
Async XLA Ops:
  0.6 0.8 copy-start
  2.2 8.5 %collective-permute-start = (f32[4,32,256]{2,1,0:T(8,128)S(1)}, f32[4,32,256]{2,1,0:T(8,128)S(1)}, u32[]{:S(2)}, u32[]{:S(2)}) collective-permute-start(f32[4,32,256]{2,1,0:T(8,128)S(1)} %pad_maximum_fusion.1), channel_id=1, source_target_pairs={{0,1},{1,2},{2,3},{3,4},{4,5},{5,6},{6,7},{8,9},{9,10},{10,11},{11... | collective-permute-start | bytes 393224 | tf_op jit(solution)/shard_map/ppermute | solution.py:23
  5.4 7.8 %collective-permute-start.1 = (f32[4,32,256]{2,1,0:T(8,128)S(1)}, f32[4,32,256]{2,1,0:T(8,128)S(1)}, u32[]{:S(2)}, u32[]{:S(2)}) collective-permute-start(f32[4,32,256]{2,1,0:T(8,128)S(1)} %pad_maximum_fusion.1), channel_id=1, source_target_pairs={{1,0},{2,1},{3,2},{4,3},{5,4},{6,5},{7,6},{9,8},{10,9},{11,10},{12... | collective-permute-start | bytes 393224 | tf_op jit(solution)/shard_map/ppermute | solution.py:24
  9.4 3.8 %copy-start.1 = (f32[1,32,256]{2,1,0:T(8,128)S(1)}, f32[1,32,256]{2,1,0:T(8,128)}, u32[]{:S(2)}) copy-start(f32[1,32,256]{2,1,0:T(8,128)} %param.4) | copy-start | bytes 98308
  19.4 38.7 %all-to-all-start = ((f32[2,64,256]{2,0,1:T(2,128)}), f32[2,64,256]{2,0,1:T(2,128)S(1)}, u32[]{:S(2)}, u32[]{:S(2)}) async-start(f32[2,64,256]{2,0,1:T(2,128)} %pad_maximum_fusion.2), calls=%async_computation | async-start | bytes 262144 | tf_op jit(solution)/shard_map/all_to_all | solution.py:134
  59.3 20.7 %all-to-all-start.1 = ((f32[1,64,256]{2,0,1:T(1,128)}), f32[1,64,256]{2,0,1:T(1,128)S(1)}, u32[]{:S(2)}, u32[]{:S(2)}) async-start(f32[1,64,256]{2,0,1:T(1,128)} %copy.32), calls=%async_computation.1 | async-start | bytes 131072 | tf_op jit(solution)/shard_map/all_to_all | solution.py:134
  85.1 20.7 %all-to-all-start.2 = ((f32[2,64,128]{2,0,1:T(2,128)}), f32[2,64,128]{2,0,1:T(2,128)S(1)}, u32[]{:S(2)}, u32[]{:S(2)}) async-start(f32[2,64,128]{2,0,1:T(2,128)} %pad_maximum_fusion.6), calls=%async_computation.2 | async-start | bytes 131072 | tf_op jit(solution)/shard_map/all_to_all | solution.py:134

commit v7 on v6

--- a/solution.py
+++ b/solution.py
@@ -54,6 +54,29 @@
     col_flux = col_w * col_diff
     divergence = (((-row_flux[:-1]) + row_flux[1:]) + (-col_flux[:, :-1])) + col_flux[:, 1:]
     diagonal = ((row_w[:-1] + row_w[1:]) + col_w[:, :-1]) + col_w[:, 1:]
+    return divergence, diagonal
+
+
+def neighbours(x):
+    padded = jnp.pad(x, ((1, 1), (1, 1)))
+    return (padded[:-2, 1:-1], padded[2:, 1:-1], padded[1:-1, :-2], padded[1:-1, 2:])
+
+
+def neighbour_faces(reluctivity, saturation):
+    rel_faces = [0.5 * (reluctivity + other) for other in neighbours(reluctivity)]
+    sat_faces = [0.5 * (saturation + other) for other in neighbours(saturation)]
+    return list(zip(rel_faces, sat_faces))
+
+
+def cell_terms(field, faces):
+    divergence = jnp.zeros_like(field)
+    diagonal = jnp.zeros_like(field)
+    for other, (face_rel, face_sat) in zip(neighbours(field), faces):
+        difference = other - field
+        square = difference * difference
+        weight = face_rel * (1.0 + face_sat * square / (1.0 + square))
+        divergence = divergence + weight * difference
+        diagonal = diagonal + weight
     return divergence, diagonal
 
 
@@ -157,15 +180,12 @@
     keep_map = slice_index != cut_slice
 
     def fine_solve(values, low, high):
-        row_rel = face_terms(reluct[low:high], 0)
-        row_sat = face_terms(satur[low:high], 0)
-        col_rel = face_terms(reluct[low:high], 1)
-        col_sat = face_terms(satur[low:high], 1)
+        faces = neighbour_faces(reluct[low:high], satur[low:high])
         mobile_ext = mobile_all[low:high]
         src_cos, src_sin = cos_all[low:high], sin_all[low:high]
 
         def single_step(values, step_index):
-            divergence, diagonal = flux_terms(values, row_rel, row_sat, col_rel, col_sat)
+            divergence, diagonal = cell_terms(values, faces)
             phase_angle = (slice_index * FINE + step_index).astype(jnp.float32) * scale
             current = src_cos * jnp.cos(phase_angle) + src_sin * jnp.sin(phase_angle)
             return values + mobile_ext * (divergence + current), diagonal

time: 127 us -> 123 us (0.969)
  blocking collectives: 19.7 us -> 58.2 us
  starting transfers between devices: 34.2 us -> 14.1 us
  waiting for transfers between devices: 53.6 us -> 34.6 us
  other arithmetic: 12.1 us -> 9.36 us
    all_to_all x1 -> x2, blocking collectives: 19.7 us -> 58.2 us  [exchange(): return lax.all_to_all(parts, 'tm', 1, 1, tiled=True)]
    all_to_all x3 -> x2, starting transfers between devices: 28.9 us -> 8.87 us  [exchange(): return lax.all_to_all(parts, 'tm', 1, 1, tiled=True)]
    all_to_all x3 -> x2, waiting for transfers between devices: 51.1 us -> 32.1 us  [exchange(): return lax.all_to_all(parts, 'tm', 1, 1, tiled=True)]
    mul x64 -> x3, other arithmetic: 5.32 us -> 0.56 us  [cell_terms(): weight = face_rel * (1.0 + face_sat * square / (1.0 + square))]
    add x30 -> x31, other arithmetic: 2.93 us -> 5.72 us  [single_step(): return (values + mobile_ext * (divergence + current), diagonal)]
  transfers between devices with their start and end apart: 5 -> 4, of which waited for: 4 -> 3; matrix products, arithmetic and copies ran while one was open for 0% -> 0% of each run, Pallas kernels for 0% -> 0%
where the time goes in v7:
time: 123 us
  blocking collectives  58.2 us (47%)
  waiting for transfers between devices  34.6 us (28%)
  starting transfers between devices  14.1 us (11%)
  other arithmetic  9.36 us (8%)
  between operations  4.4 us (4%)
  local copies, waits for them, and re-layouts  2 us (2%)
    all_to_all x2, blocking collectives, exchange(): return lax.all_to_all(parts, 'tm', 1, 1, tiled=True)  58.2 us
    all_to_all x2, waiting for transfers between devices, exchange(): return lax.all_to_all(parts, 'tm', 1, 1, tiled=True)  32.1 us
    all_to_all x2, starting transfers between devices, exchange(): return lax.all_to_all(parts, 'tm', 1, 1, tiled=True)  8.87 us
    add x31, other arithmetic, single_step(): return (values + mobile_ext * (divergence + current), diagonal)  5.72 us
    ppermute x1, starting transfers between devices, with_halo(): lax.ppermute(lax.slice_in_dim(block, rows - width, rows, axis=block.ndim...  3.12 us
    ppermute x1, waiting for transfers between devices, with_halo(): lax.ppermute(lax.slice_in_dim(block, 0, width, axis=block.ndim - 2), 'spa...  2.48 us
  transfers between devices with their start and end apart: 4, of which 3 were waited for; matrix products, arithmetic and copies ran while one was open for 0% of the time, Pallas kernels for 0%

profile of v7, /device:TPU:7, one launch (start us, length us, event | category | flops | bytes accessed | tf_op | source)
XLA Modules:
  0.0 122.8 jit_solution(6646690810966838683)
XLA Ops:
  0.6 0.8 add_bitcast_fusion.2
  1.5 0.8 pad_maximum_fusion.1
  2.2 3.1 %collective-permute-start = (f32[4,32,256]{2,1,0:T(8,128)S(1)}, f32[4,32,256]{2,1,0:T(8,128)S(1)}, u32[]{:S(2)}, u32[]{:S(2)}) collective-permute-start(f32[4,32,256]{2,1,0:T(8,128)S(1)} %pad_maximum_fusion.1), channel_id=1, source_target_pairs={{0,1},{1,2},{2,3},{3,4},{4,5},{5,6},{6,7},{8,9},{9,10},{10,11},{11... | collective-permute-start | bytes 393224 | tf_op jit(solution)/shard_map/ppermute | solution.py:23
  5.4 2.2 %collective-permute-start.1 = (f32[4,32,256]{2,1,0:T(8,128)S(1)}, f32[4,32,256]{2,1,0:T(8,128)S(1)}, u32[]{:S(2)}, u32[]{:S(2)}) collective-permute-start(f32[4,32,256]{2,1,0:T(8,128)S(1)} %pad_maximum_fusion.1), channel_id=1, source_target_pairs={{1,0},{2,1},{3,2},{4,3},{5,4},{6,5},{7,6},{9,8},{10,9},{11,10},{12... | collective-permute-start | bytes 393224 | tf_op jit(solution)/shard_map/ppermute | solution.py:24
  10.7 2.5 %collective-permute-done.1 = f32[4,32,256]{2,1,0:T(8,128)S(1)} collective-permute-done((f32[4,32,256]{2,1,0:T(8,128)S(1)}, f32[4,32,256]{2,1,0:T(8,128)S(1)}, u32[]{:S(2)}, u32[]{:S(2)}) %collective-permute-start.1) | collective-permute-done | bytes 131104 | tf_op jit(solution)/shard_map/ppermute | solution.py:24
  13.4 0.3 fusion.109
  13.8 0.2 fusion.107
  14.0 0.2 fusion.105
  14.2 0.2 fusion.103
  14.5 0.2 fusion.101
  14.7 0.2 fusion.99
  15.0 0.2 fusion.97
  15.2 0.2 fusion.95
  15.4 0.2 fusion.93
  15.7 0.2 fusion.91
  15.9 0.2 fusion.89
  16.1 0.2 fusion.87
  16.4 0.2 fusion.85
  16.6 0.2 fusion.83
  16.8 0.2 fusion.81
  17.1 0.3 add_multiply_fusion
  17.6 0.1 pad_maximum_fusion.2
  17.8 38.5 %all_to_all.20 = f32[2,64,256]{2,0,1:T(2,128)S(1)} all-to-all(f32[2,64,256]{2,0,1:T(2,128)S(1)} %pad_maximum_fusion.2), channel_id=1, replica_groups=mesh['tm'=64,'space'=8] {'tm'}, dimensions={1} | all-to-all | bytes 262144 | tf_op jit(solution)/shard_map/all_to_all | solution.py:157
  56.8 0.7 copy.32
  57.5 4.4 %all-to-all-start.1 = ((f32[1,64,256]{2,0,1:T(1,128)}), f32[1,64,256]{2,0,1:T(1,128)S(1)}, u32[]{:S(2)}, u32[]{:S(2)}) async-start(f32[1,64,256]{2,0,1:T(1,128)} %copy.32), calls=%async_computation.1 | async-start | bytes 131072 | tf_op jit(solution)/shard_map/all_to_all | solution.py:157
  62.0 16.1 %all-to-all-done.1 = f32[1,64,256]{2,0,1:T(1,128)S(1)} async-done(((f32[1,64,256]{2,0,1:T(1,128)}), f32[1,64,256]{2,0,1:T(1,128)S(1)}, u32[]{:S(2)}, u32[]{:S(2)}) %all-to-all-start.1) | async-done | bytes 65568 | tf_op jit(solution)/shard_map/all_to_all | solution.py:157
  78.1 0.2 add_multiply_fusion.6
  78.2 0.1 fusion.227
  78.4 0.1 fusion.225
  78.5 0.1 fusion.223
  78.7 0.1 fusion.221
  78.8 0.1 fusion.219
  78.9 0.1 fusion.217
  79.1 0.1 fusion.215
  79.2 0.1 fusion.213
  79.4 0.1 fusion.211
  79.5 0.1 fusion.209
  79.6 0.1 fusion.207
  79.8 0.1 fusion.205
  79.9 0.1 fusion.203
  80.1 0.1 fusion.201
  80.2 0.1 fusion.199
  80.3 0.1 add_multiply_fusion.5
  80.5 0.7 pad_maximum_fusion.6
  81.2 4.4 %all-to-all-start.2 = ((f32[2,64,128]{2,0,1:T(2,128)}), f32[2,64,128]{2,0,1:T(2,128)S(1)}, u32[]{:S(2)}, u32[]{:S(2)}) async-start(f32[2,64,128]{2,0,1:T(2,128)} %pad_maximum_fusion.6), calls=%async_computation.2 | async-start | bytes 131072 | tf_op jit(solution)/shard_map/all_to_all | solution.py:157
  85.7 16.1 %all-to-all-done.2 = f32[2,64,128]{2,0,1:T(2,128)S(1)} async-done(((f32[2,64,128]{2,0,1:T(2,128)}), f32[2,64,128]{2,0,1:T(2,128)S(1)}, u32[]{:S(2)}, u32[]{:S(2)}) %all-to-all-start.2) | async-done | bytes 65568 | tf_op jit(solution)/shard_map/all_to_all | solution.py:157
  102.3 19.7 %all_to_all.21 = f32[2,64,128]{2,0,1:T(2,128)S(1)} all-to-all(f32[2,64,128]{2,0,1:T(2,128)S(1)} %copy.38), channel_id=1, replica_groups=mesh['tm'=64,'space'=8] {'tm'}, dimensions={1} | all-to-all | bytes 131072 | tf_op jit(solution)/shard_map/all_to_all | solution.py:157
  122.1 0.7 fusion.275
  (75 shorter events, 1.4 us)
Async XLA Ops:
  0.6 0.8 copy-start
  2.2 8.5 %collective-permute-start = (f32[4,32,256]{2,1,0:T(8,128)S(1)}, f32[4,32,256]{2,1,0:T(8,128)S(1)}, u32[]{:S(2)}, u32[]{:S(2)}) collective-permute-start(f32[4,32,256]{2,1,0:T(8,128)S(1)} %pad_maximum_fusion.1), channel_id=1, source_target_pairs={{0,1},{1,2},{2,3},{3,4},{4,5},{5,6},{6,7},{8,9},{9,10},{10,11},{11... | collective-permute-start | bytes 393224 | tf_op jit(solution)/shard_map/ppermute | solution.py:23
  5.4 7.8 %collective-permute-start.1 = (f32[4,32,256]{2,1,0:T(8,128)S(1)}, f32[4,32,256]{2,1,0:T(8,128)S(1)}, u32[]{:S(2)}, u32[]{:S(2)}) collective-permute-start(f32[4,32,256]{2,1,0:T(8,128)S(1)} %pad_maximum_fusion.1), channel_id=1, source_target_pairs={{1,0},{2,1},{3,2},{4,3},{5,4},{6,5},{7,6},{9,8},{10,9},{11,10},{12... | collective-permute-start | bytes 393224 | tf_op jit(solution)/shard_map/ppermute | solution.py:24
  9.4 3.8 %copy-start.1 = (f32[1,32,256]{2,1,0:T(8,128)S(1)}, f32[1,32,256]{2,1,0:T(8,128)}, u32[]{:S(2)}) copy-start(f32[1,32,256]{2,1,0:T(8,128)} %param.4) | copy-start | bytes 98308
  57.5 20.5 %all-to-all-start.1 = ((f32[1,64,256]{2,0,1:T(1,128)}), f32[1,64,256]{2,0,1:T(1,128)S(1)}, u32[]{:S(2)}, u32[]{:S(2)}) async-start(f32[1,64,256]{2,0,1:T(1,128)} %copy.32), calls=%async_computation.1 | async-start | bytes 131072 | tf_op jit(solution)/shard_map/all_to_all | solution.py:157
  81.2 20.5 %all-to-all-start.2 = ((f32[2,64,128]{2,0,1:T(2,128)}), f32[2,64,128]{2,0,1:T(2,128)S(1)}, u32[]{:S(2)}, u32[]{:S(2)}) async-start(f32[2,64,128]{2,0,1:T(2,128)} %pad_maximum_fusion.6), calls=%async_computation.2 | async-start | bytes 131072 | tf_op jit(solution)/shard_map/all_to_all | solution.py:157

commit v8 on v7

--- a/solution.py
+++ b/solution.py
@@ -180,20 +180,22 @@
     keep_map = slice_index != cut_slice
 
     def fine_solve(values, low, high):
-        faces = neighbour_faces(reluct[low:high], satur[low:high])
-        mobile_ext = mobile_all[low:high]
-        src_cos, src_sin = cos_all[low:high], sin_all[low:high]
-
-        def single_step(values, step_index):
+        def single_step(values, step_index, trim):
+            window = slice(low + trim, high - trim)
+            faces = neighbour_faces(reluct[window], satur[window])
             divergence, diagonal = cell_terms(values, faces)
             phase_angle = (slice_index * FINE + step_index).astype(jnp.float32) * scale
-            current = src_cos * jnp.cos(phase_angle) + src_sin * jnp.sin(phase_angle)
-            return values + mobile_ext * (divergence + current), diagonal
-
-        fine_values, fine_diagonal = single_step(values, 0)
+            current = cos_all[window] * jnp.cos(phase_angle) + sin_all[window] * jnp.sin(phase_angle)
+            return values + mobile_all[window] * (divergence + current), diagonal
+
+        fine_values, fine_diagonal = single_step(values, 0, 0)
+        trim = 0
         for step_index in range(1, FINE):
-            fine_values = single_step(fine_values, step_index)[0]
-        fine_values = fine_values[FINE : high - low - FINE]
+            if step_index >= trim + 8:
+                trim += 8
+                fine_values = fine_values[8:-8]
+            fine_values = single_step(fine_values, step_index, trim)[0]
+        fine_values = fine_values[FINE - trim : high - low - FINE - trim]
         fine_diagonal = fine_diagonal[FINE : high - low - FINE]
         mobile = mobile_all[low + FINE : high - FINE]
         decay = 1.0 / (1.0 + FINE * mobile * fine_diagonal)

time: 123 us -> 124 us (level)
  blocking collectives: 58.2 us -> 19.7 us
  starting transfers between devices: 14.1 us -> 34.2 us
  waiting for transfers between devices: 34.6 us -> 53.5 us
    all_to_all x2 -> x1, blocking collectives: 58.2 us -> 19.7 us  [exchange(): return lax.all_to_all(parts, 'tm', 1, 1, tiled=True)]
    all_to_all x2 -> x3, starting transfers between devices: 8.87 us -> 29 us  [exchange(): return lax.all_to_all(parts, 'tm', 1, 1, tiled=True)]
    all_to_all x2 -> x3, waiting for transfers between devices: 32.1 us -> 51 us  [exchange(): return lax.all_to_all(parts, 'tm', 1, 1, tiled=True)]
  transfers between devices with their start and end apart: 4 -> 5, of which waited for: 3 -> 4; matrix products, arithmetic and copies ran while one was open for 0% -> 0% of each run, Pallas kernels for 0% -> 0%
where the time goes in v8:
time: 124 us; the launch traced here: 123 us
  waiting for transfers between devices  53.5 us (43%)
  starting transfers between devices  34.2 us (28%)
  blocking collectives  19.7 us (16%)
  other arithmetic  9.46 us (8%)
  between operations  4.5 us (4%)
  local copies, waits for them, and re-layouts  2.03 us (2%)
    all_to_all x3, waiting for transfers between devices, exchange(): return lax.all_to_all(parts, 'tm', 1, 1, tiled=True)  51 us
    all_to_all x3, starting transfers between devices, exchange(): return lax.all_to_all(parts, 'tm', 1, 1, tiled=True)  29 us
    all_to_all x1, blocking collectives, exchange(): return lax.all_to_all(parts, 'tm', 1, 1, tiled=True)  19.7 us
    add x31, other arithmetic, single_step(): return (values + mobile_all[window] * (divergence + current), diagonal)  4.86 us
    ppermute x1, starting transfers between devices, with_halo(): lax.ppermute(lax.slice_in_dim(block, rows - width, rows, axis=block.ndim...  3.12 us
  transfers between devices with their start and end apart: 5, of which 4 were waited for; matrix products, arithmetic and copies ran while one was open for 0% of the time, Pallas kernels for 0%

profile of v8, /device:TPU:7, one launch (start us, length us, event | category | flops | bytes accessed | tf_op | source)
XLA Modules:
  0.0 123.5 jit_solution(9982545179832925235)
XLA Ops:
  0.6 0.8 add_bitcast_fusion.4
  1.5 0.8 pad_maximum_fusion.1
  2.2 3.1 %collective-permute-start = (f32[4,32,256]{2,1,0:T(8,128)S(1)}, f32[4,32,256]{2,1,0:T(8,128)S(1)}, u32[]{:S(2)}, u32[]{:S(2)}) collective-permute-start(f32[4,32,256]{2,1,0:T(8,128)S(1)} %pad_maximum_fusion.1), channel_id=1, source_target_pairs={{0,1},{1,2},{2,3},{3,4},{4,5},{5,6},{6,7},{8,9},{9,10},{10,11},{11... | collective-permute-start | bytes 393224 | tf_op jit(solution)/shard_map/ppermute | solution.py:23
  5.4 2.2 %collective-permute-start.1 = (f32[4,32,256]{2,1,0:T(8,128)S(1)}, f32[4,32,256]{2,1,0:T(8,128)S(1)}, u32[]{:S(2)}, u32[]{:S(2)}) collective-permute-start(f32[4,32,256]{2,1,0:T(8,128)S(1)} %pad_maximum_fusion.1), channel_id=1, source_target_pairs={{1,0},{2,1},{3,2},{4,3},{5,4},{6,5},{7,6},{9,8},{10,9},{11,10},{12... | collective-permute-start | bytes 393224 | tf_op jit(solution)/shard_map/ppermute | solution.py:24
  10.7 2.5 %collective-permute-done.1 = f32[4,32,256]{2,1,0:T(8,128)S(1)} collective-permute-done((f32[4,32,256]{2,1,0:T(8,128)S(1)}, f32[4,32,256]{2,1,0:T(8,128)S(1)}, u32[]{:S(2)}, u32[]{:S(2)}) %collective-permute-start.1) | collective-permute-done | bytes 131104 | tf_op jit(solution)/shard_map/ppermute | solution.py:24
  13.4 0.3 fusion.61
  13.8 0.2 fusion.59
  14.0 0.2 fusion.57
  14.3 0.2 fusion.55
  14.5 0.2 fusion.53
  14.7 0.2 fusion.51
  15.0 0.2 fusion.49
  15.2 0.3 add_multiply_fusion
  15.5 0.2 fusion.125
  15.8 0.1 fusion.123
  15.9 0.1 fusion.121
  16.1 0.1 fusion.119
  16.3 0.1 fusion.117
  16.4 0.1 fusion.115
  16.6 0.1 fusion.113
  16.7 0.1 add_multiply_fusion.5
  17.2 0.8 pad_maximum_fusion.2
  18.0 20.1 %all-to-all-start = ((f32[2,64,256]{2,0,1:T(2,128)}), f32[2,64,256]{2,0,1:T(2,128)S(1)}, u32[]{:S(2)}, u32[]{:S(2)}) async-start(f32[2,64,256]{2,0,1:T(2,128)} %pad_maximum_fusion.2), calls=%async_computation | async-start | bytes 262144 | tf_op jit(solution)/shard_map/all_to_all | solution.py:157
  38.1 18.6 %all-to-all-done = f32[2,64,256]{2,0,1:T(2,128)S(1)} async-done(((f32[2,64,256]{2,0,1:T(2,128)}), f32[2,64,256]{2,0,1:T(2,128)S(1)}, u32[]{:S(2)}, u32[]{:S(2)}) %all-to-all-start) | async-done | bytes 131104 | tf_op jit(solution)/shard_map/all_to_all | solution.py:157
  57.2 0.7 copy.32
  57.9 4.4 %all-to-all-start.1 = ((f32[1,64,256]{2,0,1:T(1,128)}), f32[1,64,256]{2,0,1:T(1,128)S(1)}, u32[]{:S(2)}, u32[]{:S(2)}) async-start(f32[1,64,256]{2,0,1:T(1,128)} %copy.32), calls=%async_computation.1 | async-start | bytes 131072 | tf_op jit(solution)/shard_map/all_to_all | solution.py:157
  62.4 16.2 %all-to-all-done.1 = f32[1,64,256]{2,0,1:T(1,128)S(1)} async-done(((f32[1,64,256]{2,0,1:T(1,128)}), f32[1,64,256]{2,0,1:T(1,128)S(1)}, u32[]{:S(2)}, u32[]{:S(2)}) %all-to-all-start.1) | async-done | bytes 65568 | tf_op jit(solution)/shard_map/all_to_all | solution.py:157
  78.6 0.2 add_multiply_fusion.7
  78.8 0.1 fusion.195
  79.0 0.1 fusion.193
  79.1 0.1 fusion.191
  79.3 0.1 fusion.189
  79.4 0.1 fusion.187
  79.5 0.1 fusion.185
  79.7 0.1 fusion.183
  79.8 0.1 add_multiply_fusion.6
  80.0 0.2 fusion.259
  80.1 0.1 fusion.257
  80.3 0.1 fusion.255
  80.4 0.1 fusion.253
  80.5 0.1 fusion.251
  80.6 0.1 fusion.249
  80.8 0.1 fusion.247
  81.1 0.7 pad_maximum_fusion.6
  81.8 4.4 %all-to-all-start.2 = ((f32[2,64,128]{2,0,1:T(2,128)}), f32[2,64,128]{2,0,1:T(2,128)S(1)}, u32[]{:S(2)}, u32[]{:S(2)}) async-start(f32[2,64,128]{2,0,1:T(2,128)} %pad_maximum_fusion.6), calls=%async_computation.2 | async-start | bytes 131072 | tf_op jit(solution)/shard_map/all_to_all | solution.py:157
  86.2 16.3 %all-to-all-done.2 = f32[2,64,128]{2,0,1:T(2,128)S(1)} async-done(((f32[2,64,128]{2,0,1:T(2,128)}), f32[2,64,128]{2,0,1:T(2,128)S(1)}, u32[]{:S(2)}, u32[]{:S(2)}) %all-to-all-start.2) | async-done | bytes 65568 | tf_op jit(solution)/shard_map/all_to_all | solution.py:157
  103.1 19.7 %all_to_all.20 = f32[2,64,128]{2,0,1:T(2,128)S(1)} all-to-all(f32[2,64,128]{2,0,1:T(2,128)S(1)} %copy.38), channel_id=1, replica_groups=mesh['tm'=64,'space'=8] {'tm'}, dimensions={1} | all-to-all | bytes 131072 | tf_op jit(solution)/shard_map/all_to_all | solution.py:157
  122.8 0.7 fusion.327
  (83 shorter events, 1.7 us)
Async XLA Ops:
  0.6 0.8 copy-start
  2.2 8.5 %collective-permute-start = (f32[4,32,256]{2,1,0:T(8,128)S(1)}, f32[4,32,256]{2,1,0:T(8,128)S(1)}, u32[]{:S(2)}, u32[]{:S(2)}) collective-permute-start(f32[4,32,256]{2,1,0:T(8,128)S(1)} %pad_maximum_fusion.1), channel_id=1, source_target_pairs={{0,1},{1,2},{2,3},{3,4},{4,5},{5,6},{6,7},{8,9},{9,10},{10,11},{11... | collective-permute-start | bytes 393224 | tf_op jit(solution)/shard_map/ppermute | solution.py:23
  5.4 7.8 %collective-permute-start.1 = (f32[4,32,256]{2,1,0:T(8,128)S(1)}, f32[4,32,256]{2,1,0:T(8,128)S(1)}, u32[]{:S(2)}, u32[]{:S(2)}) collective-permute-start(f32[4,32,256]{2,1,0:T(8,128)S(1)} %pad_maximum_fusion.1), channel_id=1, source_target_pairs={{1,0},{2,1},{3,2},{4,3},{5,4},{6,5},{7,6},{9,8},{10,9},{11,10},{12... | collective-permute-start | bytes 393224 | tf_op jit(solution)/shard_map/ppermute | solution.py:24
  9.4 3.8 %copy-start.1 = (f32[1,32,256]{2,1,0:T(8,128)S(1)}, f32[1,32,256]{2,1,0:T(8,128)}, u32[]{:S(2)}) copy-start(f32[1,32,256]{2,1,0:T(8,128)} %param.4) | copy-start | bytes 98308
  18.0 38.7 %all-to-all-start = ((f32[2,64,256]{2,0,1:T(2,128)}), f32[2,64,256]{2,0,1:T(2,128)S(1)}, u32[]{:S(2)}, u32[]{:S(2)}) async-start(f32[2,64,256]{2,0,1:T(2,128)} %pad_maximum_fusion.2), calls=%async_computation | async-start | bytes 262144 | tf_op jit(solution)/shard_map/all_to_all | solution.py:157
  57.9 20.7 %all-to-all-start.1 = ((f32[1,64,256]{2,0,1:T(1,128)}), f32[1,64,256]{2,0,1:T(1,128)S(1)}, u32[]{:S(2)}, u32[]{:S(2)}) async-start(f32[1,64,256]{2,0,1:T(1,128)} %copy.32), calls=%async_computation.1 | async-start | bytes 131072 | tf_op jit(solution)/shard_map/all_to_all | solution.py:157
  81.8 20.7 %all-to-all-start.2 = ((f32[2,64,128]{2,0,1:T(2,128)}), f32[2,64,128]{2,0,1:T(2,128)S(1)}, u32[]{:S(2)}, u32[]{:S(2)}) async-start(f32[2,64,128]{2,0,1:T(2,128)} %pad_maximum_fusion.6), calls=%async_computation.2 | async-start | bytes 131072 | tf_op jit(solution)/shard_map/all_to_all | solution.py:157

commit v9 on v7

--- a/solution.py
+++ b/solution.py
@@ -228,13 +228,12 @@
     field_block = from_chunks(exchange(states_timed[None])[0])
 
     fine_end, decay = fine_solve(field_block, width, rows + 3 * width)
+    previous_end = lax.ppermute(fine_end, "tm", [(i, (i + 1) % slices) for i in range(slices)])
     timed = exchange(jnp.stack([cells_of(decay), cells_of(fine_end)]))
     offset_timed = timed[1] - timed[0] * strip_timed
     states_timed = scan_over_time(timed[0], offset_timed)
-    ends_timed = timed[1]
-    jumps_timed = jnp.concatenate([ends_timed[slices - 1 :], ends_timed[: slices - 1]], 0) - states_timed
-    back = exchange(jnp.stack([states_timed, jumps_timed]))
-    return (grid_of(back[0])[None], grid_of(back[1])[None])
+    states = grid_of(lax.all_to_all(states_timed, "tm", 0, 0, tiled=True))
+    return (states[None], (previous_end - states)[None])
 
 
 def solution(mesh):

time: 123 us -> 124 us (level)
  blocking collectives: 58.2 us -> 38.5 us
  waiting for transfers between devices: 34.6 us -> 44.3 us
  starting transfers between devices: 14.1 us -> 23.6 us
  other arithmetic: 9.36 us -> 10.6 us
    all_to_all x2 -> x1, blocking collectives: 58.2 us -> 38.5 us  [exchange(): return lax.all_to_all(parts, 'tm', 1, 1, tiled=True)]
    all_to_all x0 -> x1, waiting for transfers between devices: none -> 9.67 us  [on_device(): states = grid_of(lax.all_to_all(states_timed, 'tm', 0, 0, tiled=True))]
    ppermute x0 -> x1, starting transfers between devices: none -> 5.05 us  [on_device(): lax.ppermute(fine_end, 'tm', [(i, (i + 1) % slices) for i in range(slices)])]
    all_to_all x0 -> x1, starting transfers between devices: none -> 4.42 us  [on_device(): states = grid_of(lax.all_to_all(states_timed, 'tm', 0, 0, tiled=True))]
  transfers between devices with their start and end apart: 4 -> 6, of which waited for: 3 -> 4; matrix products, arithmetic and copies ran while one was open for 0% -> 0% of each run, Pallas kernels for 0% -> 0%
where the time goes in v9:
time: 124 us; the launch traced here: 123 us
  waiting for transfers between devices  44.3 us (36%)
  blocking collectives  38.5 us (31%)
  starting transfers between devices  23.6 us (19%)
  other arithmetic  10.6 us (9%)
  between operations  4.38 us (4%)
  local copies, waits for them, and re-layouts  1.84 us (1%)
    all_to_all x1, blocking collectives, exchange(): return lax.all_to_all(parts, 'tm', 1, 1, tiled=True)  38.5 us
    all_to_all x2, waiting for transfers between devices, exchange(): return lax.all_to_all(parts, 'tm', 1, 1, tiled=True)  32.1 us
    all_to_all x1, waiting for transfers between devices, on_device(): states = grid_of(lax.all_to_all(states_timed, 'tm', 0, 0, tiled=True))  9.67 us
    all_to_all x2, starting transfers between devices, exchange(): return lax.all_to_all(parts, 'tm', 1, 1, tiled=True)  8.87 us
    add x31, other arithmetic, single_step(): return (values + mobile_ext * (divergence + current), diagonal)  5.72 us
    ppermute x1, starting transfers between devices, on_device(): lax.ppermute(fine_end, 'tm', [(i, (i + 1) % slices) for i in range(slices)])  5.05 us
    all_to_all x1, starting transfers between devices, on_device(): states = grid_of(lax.all_to_all(states_timed, 'tm', 0, 0, tiled=True))  4.42 us
    ppermute x1, starting transfers between devices, with_halo(): lax.ppermute(lax.slice_in_dim(block, rows - width, rows, axis=block.ndim...  3.12 us
  transfers between devices with their start and end apart: 6, of which 4 were waited for; matrix products, arithmetic and copies ran while one was open for 0% of the time, Pallas kernels for 0%

profile of v9, /device:TPU:7, one launch (start us, length us, event | category | flops | bytes accessed | tf_op | source)
XLA Modules:
  0.0 123.2 jit_solution(6981354748229032484)
XLA Ops:
  0.6 0.8 add_bitcast_fusion.2
  1.5 0.8 pad_maximum_fusion.1
  2.2 3.1 %collective-permute-start = (f32[4,32,256]{2,1,0:T(8,128)S(1)}, f32[4,32,256]{2,1,0:T(8,128)S(1)}, u32[]{:S(2)}, u32[]{:S(2)}) collective-permute-start(f32[4,32,256]{2,1,0:T(8,128)S(1)} %pad_maximum_fusion.1), channel_id=1, source_target_pairs={{0,1},{1,2},{2,3},{3,4},{4,5},{5,6},{6,7},{8,9},{9,10},{10,11},{11... | collective-permute-start | bytes 393224 | tf_op jit(solution)/shard_map/ppermute | solution.py:23
  5.4 2.2 %collective-permute-start.1 = (f32[4,32,256]{2,1,0:T(8,128)S(1)}, f32[4,32,256]{2,1,0:T(8,128)S(1)}, u32[]{:S(2)}, u32[]{:S(2)}) collective-permute-start(f32[4,32,256]{2,1,0:T(8,128)S(1)} %pad_maximum_fusion.1), channel_id=1, source_target_pairs={{1,0},{2,1},{3,2},{4,3},{5,4},{6,5},{7,6},{9,8},{10,9},{11,10},{12... | collective-permute-start | bytes 393224 | tf_op jit(solution)/shard_map/ppermute | solution.py:24
  10.7 2.5 %collective-permute-done.1 = f32[4,32,256]{2,1,0:T(8,128)S(1)} collective-permute-done((f32[4,32,256]{2,1,0:T(8,128)S(1)}, f32[4,32,256]{2,1,0:T(8,128)S(1)}, u32[]{:S(2)}, u32[]{:S(2)}) %collective-permute-start.1) | collective-permute-done | bytes 131104 | tf_op jit(solution)/shard_map/ppermute | solution.py:24
  13.4 0.3 fusion.109
  13.8 0.2 fusion.107
  14.0 0.2 fusion.105
  14.2 0.2 fusion.103
  14.5 0.2 fusion.101
  14.7 0.2 fusion.99
  15.0 0.2 fusion.97
  15.2 0.2 fusion.95
  15.4 0.2 fusion.93
  15.7 0.2 fusion.91
  15.9 0.2 fusion.89
  16.1 0.2 fusion.87
  16.4 0.2 fusion.85
  16.6 0.2 fusion.83
  16.8 0.2 fusion.81
  17.1 0.3 add_multiply_fusion
  17.8 38.5 %all_to_all.21 = f32[2,64,256]{2,0,1:T(2,128)S(1)} all-to-all(f32[2,64,256]{2,0,1:T(2,128)S(1)} %pad_maximum_fusion.2), channel_id=1, replica_groups=mesh['tm'=64,'space'=8] {'tm'}, dimensions={1} | all-to-all | bytes 262144 | tf_op jit(solution)/shard_map/all_to_all | solution.py:157
  56.8 0.7 copy.30
  57.5 4.4 %all-to-all-start.1 = ((f32[1,64,256]{2,0,1:T(1,128)}), f32[1,64,256]{2,0,1:T(1,128)S(1)}, u32[]{:S(2)}, u32[]{:S(2)}) async-start(f32[1,64,256]{2,0,1:T(1,128)} %copy.30), calls=%async_computation.1 | async-start | bytes 131072 | tf_op jit(solution)/shard_map/all_to_all | solution.py:157
  62.0 16.1 %all-to-all-done.1 = f32[1,64,256]{2,0,1:T(1,128)S(1)} async-done(((f32[1,64,256]{2,0,1:T(1,128)}), f32[1,64,256]{2,0,1:T(1,128)S(1)}, u32[]{:S(2)}, u32[]{:S(2)}) %all-to-all-start.1) | async-done | bytes 65568 | tf_op jit(solution)/shard_map/all_to_all | solution.py:157
  78.1 0.2 add_multiply_fusion.6
  78.2 0.1 fusion.227
  78.4 0.1 fusion.225
  78.5 0.1 fusion.223
  78.7 0.1 fusion.221
  78.8 0.1 fusion.219
  78.9 0.1 fusion.217
  79.1 0.1 fusion.215
  79.2 0.1 fusion.213
  79.4 0.1 fusion.211
  79.5 0.1 fusion.209
  79.6 0.1 fusion.207
  79.8 0.1 fusion.205
  79.9 0.1 fusion.203
  80.5 0.7 pad_maximum_fusion.6
  81.2 4.4 %all-to-all-start.2 = ((f32[2,64,128]{2,0,1:T(2,128)}), f32[2,64,128]{2,0,1:T(2,128)S(1)}, u32[]{:S(2)}, u32[]{:S(2)}) async-start(f32[2,64,128]{2,0,1:T(2,128)} %pad_maximum_fusion.6), calls=%async_computation.2 | async-start | bytes 131072 | tf_op jit(solution)/shard_map/all_to_all | solution.py:157
  85.7 16.1 %all-to-all-done.2 = f32[2,64,128]{2,0,1:T(2,128)S(1)} async-done(((f32[2,64,128]{2,0,1:T(2,128)}), f32[2,64,128]{2,0,1:T(2,128)S(1)}, u32[]{:S(2)}, u32[]{:S(2)}) %all-to-all-start.2) | async-done | bytes 65568 | tf_op jit(solution)/shard_map/all_to_all | solution.py:157
  102.2 0.6 bitcast_add_fusion.30
  102.8 4.4 %all-to-all-start.3 = ((f32[64,1,128]{2,1,0:T(1,128)}), f32[64,1,128]{2,1,0:T(1,128)S(1)}, u32[]{:S(2)}, u32[]{:S(2)}) async-start(f32[64,1,128]{2,1,0:T(1,128)} %bitcast.94), calls=%async_computation.3 | async-start | bytes 65536 | tf_op jit(solution)/shard_map/all_to_all | solution.py:235
  107.3 5.1 %collective-permute-start.2 = (f32[32,256]{1,0:T(8,128)S(1)}, f32[32,256]{1,0:T(8,128)S(1)}, u32[]{:S(2)}, u32[]{:S(2)}) collective-permute-start(f32[32,256]{1,0:T(8,128)S(1)} %slice_add_fusion.7), channel_id=1, source_target_pairs={{0,8},{8,16},{16,24},{24,32},{32,40},{40,48},{48,56},{56,64},{64,7... | collective-permute-start | bytes 98312 | tf_op jit(solution)/shard_map/ppermute | solution.py:231
  112.3 9.7 %all-to-all-done.3 = f32[64,1,128]{2,1,0:T(1,128)S(1)} async-done(((f32[64,1,128]{2,1,0:T(1,128)}), f32[64,1,128]{2,1,0:T(1,128)S(1)}, u32[]{:S(2)}, u32[]{:S(2)}) %all-to-all-start.3) | async-done | bytes 32800 | tf_op jit(solution)/shard_map/all_to_all | solution.py:235
  122.0 0.6 subtract_bitcast_fusion
  122.6 0.6 copy.51
  (75 shorter events, 1.8 us)
Async XLA Ops:
  0.6 0.8 copy-start
  2.2 8.5 %collective-permute-start = (f32[4,32,256]{2,1,0:T(8,128)S(1)}, f32[4,32,256]{2,1,0:T(8,128)S(1)}, u32[]{:S(2)}, u32[]{:S(2)}) collective-permute-start(f32[4,32,256]{2,1,0:T(8,128)S(1)} %pad_maximum_fusion.1), channel_id=1, source_target_pairs={{0,1},{1,2},{2,3},{3,4},{4,5},{5,6},{6,7},{8,9},{9,10},{10,11},{11... | collective-permute-start | bytes 393224 | tf_op jit(solution)/shard_map/ppermute | solution.py:23
  5.4 7.8 %collective-permute-start.1 = (f32[4,32,256]{2,1,0:T(8,128)S(1)}, f32[4,32,256]{2,1,0:T(8,128)S(1)}, u32[]{:S(2)}, u32[]{:S(2)}) collective-permute-start(f32[4,32,256]{2,1,0:T(8,128)S(1)} %pad_maximum_fusion.1), channel_id=1, source_target_pairs={{1,0},{2,1},{3,2},{4,3},{5,4},{6,5},{7,6},{9,8},{10,9},{11,10},{12... | collective-permute-start | bytes 393224 | tf_op jit(solution)/shard_map/ppermute | solution.py:24
  9.4 3.8 %copy-start.1 = (f32[1,32,256]{2,1,0:T(8,128)S(1)}, f32[1,32,256]{2,1,0:T(8,128)}, u32[]{:S(2)}) copy-start(f32[1,32,256]{2,1,0:T(8,128)} %param.4) | copy-start | bytes 98308
  57.5 20.5 %all-to-all-start.1 = ((f32[1,64,256]{2,0,1:T(1,128)}), f32[1,64,256]{2,0,1:T(1,128)S(1)}, u32[]{:S(2)}, u32[]{:S(2)}) async-start(f32[1,64,256]{2,0,1:T(1,128)} %copy.30), calls=%async_computation.1 | async-start | bytes 131072 | tf_op jit(solution)/shard_map/all_to_all | solution.py:157
  81.2 20.5 %all-to-all-start.2 = ((f32[2,64,128]{2,0,1:T(2,128)}), f32[2,64,128]{2,0,1:T(2,128)S(1)}, u32[]{:S(2)}, u32[]{:S(2)}) async-start(f32[2,64,128]{2,0,1:T(2,128)} %pad_maximum_fusion.6), calls=%async_computation.2 | async-start | bytes 131072 | tf_op jit(solution)/shard_map/all_to_all | solution.py:157
  102.8 19.2 %all-to-all-start.3 = ((f32[64,1,128]{2,1,0:T(1,128)}), f32[64,1,128]{2,1,0:T(1,128)S(1)}, u32[]{:S(2)}, u32[]{:S(2)}) async-start(f32[64,1,128]{2,1,0:T(1,128)} %bitcast.94), calls=%async_computation.3 | async-start | bytes 65536 | tf_op jit(solution)/shard_map/all_to_all | solution.py:235
  107.3 14.7 %collective-permute-start.2 = (f32[32,256]{1,0:T(8,128)S(1)}, f32[32,256]{1,0:T(8,128)S(1)}, u32[]{:S(2)}, u32[]{:S(2)}) collective-permute-start(f32[32,256]{1,0:T(8,128)S(1)} %slice_add_fusion.7), channel_id=1, source_target_pairs={{0,8},{8,16},{16,24},{24,32},{32,40},{40,48},{48,56},{56,64},{64,7... | collective-permute-start | bytes 98312 | tf_op jit(solution)/shard_map/ppermute | solution.py:231
